TPU v7x, 32 devices: a whole 2x2x4 slice. The times are simulated.
32 devices in a mesh: head: 4 (over x, core), tok: 8 (over z, y).
Axes of the slice: x: 2, y: 2, z: 4, core: 2. Of those that a mesh axis runs over, the one named last changes fastest.
Arguments:
- tokens: bfloat16 [8, 512, 2048], P('tok', 'head'), may hold values from -6 to 6
- cache_len: int32 [8], P('tok'), may hold values from 64 to 4096, as said below
- attn_gain: float32 [2048], replicated, may hold values from 0.5 to 1.5
- w_qkv: bfloat16 [2048, 6144], P(None, 'head'), may hold values from -0.25 to 0.25
- k_cache: bfloat16 [8, 4096, 2048], P('tok', None, 'head'), may hold values from -8 to 8
- v_cache: bfloat16 [8, 4096, 2048], P('tok', None, 'head'), may hold values from -6 to 6
- w_out: bfloat16 [2048, 2048], P('head'), may hold values from -0.125 to 0.125
- moe_gain: float32 [2048], replicated, may hold values from 0.5 to 1.5
- w_shared: bfloat16 [2048, 2, 2816], P(None, None, 'head'), may hold values from -0.125 to 0.125
- w_shared_down: bfloat16 [2816, 2048], P('head'), may hold values from -0.109375 to 0.109375
- expert_ids: int32 [8, 512, 6], P('tok', 'head'), may hold values from 0 to 63, all different within a row; in each aligned block of 128 rows (0 to 127, 128 to 255, ..., all dimensions but the last counted through in order) at most 24 rows name the same one
- expert_weights: float32 [8, 512, 6], P('tok', 'head'), may hold values from 0.05 to 0.5
- expert_slot: int32 [64], replicated, may hold values from 0 to 63, each once
- w_expert: bfloat16 [2048, 2, 90112], P(None, None, ('head', 'tok')), may hold values from -0.125 to 0.125
- w_expert_down: bfloat16 [90112, 2048], P(('head', 'tok')), may hold values from -0.15625 to 0.15625
Outputs:
- layer_out: bfloat16 [8, 512, 2048], P('tok', 'head')
Inputs may be any that keep to these rules, and one draw needn't show every extreme that they name: `cache_len`: Heavy-tailed over requests; some request has exactly 4096 cached tokens and some other exactly 64. `expert_ids`: each token names 6 different experts. Rows are taken in order over requests then new tokens; in each aligned block of 128 rows no expert is named by more than 24 rows, and in some block an expert is named by exactly 24. `expert_slot`: A permutation of the experts.
All inputs are finite; a program needn't handle non-finite values.
Results may differ from a plain program's by a relative error of at most 0.014.
Values may be sent and summed in bfloat16 or wider, within the bound.
No kernel may reach another device: no remote copies, remote signals or barrier semaphores. Data moves between devices by JAX's collectives and lax.ppermute only.
A program may use at most 256 MiB of HBM per device.

v0:
```python
import math

import jax
import jax.numpy as jnp
from jax import lax
from jax.experimental import pallas as pl
from jax.experimental.pallas import tpu as pltpu
from jax.sharding import PartitionSpec as P

HD = 128
E = 64
TOP = 6


EPS = 1e-06
NEG_BIG = -1e30
CHUNKS = 2


def normalize(values, gain_vector):
    wide = values.astype(jnp.float32)
    factor = lax.rsqrt(jnp.mean(wide * wide, axis=-1, keepdims=True) + EPS)
    return (wide * factor * gain_vector).astype(jnp.bfloat16)


def rotary(vectors, positions):
    half_dim = vectors.shape[-1] // 2
    freqs = 10000.0 ** (-jnp.arange(half_dim, dtype=jnp.float32) / half_dim)
    angles = positions.astype(jnp.float32)[:, None] * freqs[None, :]
    cosine = jnp.cos(angles)[:, None, :]
    sine_part = jnp.sin(angles)[:, None, :]
    lower = vectors[..., :half_dim]
    upper = vectors[..., half_dim:]
    return jnp.concatenate(
        [lower * cosine - upper * sine_part, upper * cosine + lower * sine_part], axis=-1
    )


def attend(queries, keys_new, values_new, keys_old, values_old, length):
    factor = 1.0 / math.sqrt(queries.shape[-1])
    score_old = jnp.dot(queries, keys_old.T, preferred_element_type=jnp.float32) * factor
    score_new = jnp.dot(queries, keys_new.T, preferred_element_type=jnp.float32) * factor
    old_slots = jnp.arange(keys_old.shape[0], dtype=jnp.int32)
    live_old = (old_slots < length)[None, :]
    new_slots = jnp.arange(queries.shape[0], dtype=jnp.int32)
    live_new = new_slots[None, :] <= new_slots[:, None]
    row_max = jnp.maximum(
        jnp.max(jnp.where(live_old, score_old, NEG_BIG), axis=1),
        jnp.max(jnp.where(live_new, score_new, NEG_BIG), axis=1),
    )
    prob_old = jnp.where(live_old, jnp.exp(score_old - row_max[:, None]), 0.0)
    prob_new = jnp.where(live_new, jnp.exp(score_new - row_max[:, None]), 0.0)
    denom = jnp.sum(prob_old, axis=1) + jnp.sum(prob_new, axis=1)
    weighted = jnp.dot(
        prob_old.astype(jnp.bfloat16), values_old, preferred_element_type=jnp.float32
    )
    weighted = weighted + jnp.dot(
        prob_new.astype(jnp.bfloat16), values_new, preferred_element_type=jnp.float32
    )
    return (weighted / denom[:, None]).astype(jnp.bfloat16)


def rotate(block, cosine, sine_signed):
    half = block.shape[-1] // 2
    return block * cosine + pltpu.roll(block, half, 1) * sine_signed


def attention_kernel(
    len_ref, q_ref, kn_ref, vn_ref, cq_ref, sq_ref, ck_ref, sk_ref, ko_ref, vo_ref, o_ref
):
    rows = q_ref.shape[0]
    new_len = kn_ref.shape[0]
    cache_rows = ko_ref.shape[1]
    length = len_ref[0]
    start = pl.program_id(1) * rows
    factor = 1.0 / math.sqrt(q_ref.shape[-1])
    contract = (((1,), (1,)), ((), ()))
    queries = rotate(q_ref[...], cq_ref[...], sq_ref[...]).astype(jnp.bfloat16)
    keys_new = rotate(kn_ref[...], ck_ref[...], sk_ref[...]).astype(jnp.bfloat16)
    values_new = vn_ref[...].astype(jnp.bfloat16)
    score_old = (
        lax.dot_general(queries, ko_ref[0], contract, preferred_element_type=jnp.float32) * factor
    )
    score_new = (
        lax.dot_general(queries, keys_new, contract, preferred_element_type=jnp.float32) * factor
    )
    live_old = lax.broadcasted_iota(jnp.int32, (rows, cache_rows), 1) < length
    new_cols = lax.broadcasted_iota(jnp.int32, (rows, new_len), 1)
    new_rows = lax.broadcasted_iota(jnp.int32, (rows, new_len), 0) + start
    live_new = new_cols <= new_rows
    row_max = jnp.maximum(
        jnp.max(jnp.where(live_old, score_old, NEG_BIG), axis=1, keepdims=True),
        jnp.max(jnp.where(live_new, score_new, NEG_BIG), axis=1, keepdims=True),
    )
    prob_old = jnp.where(live_old, jnp.exp(score_old - row_max), 0.0)
    prob_new = jnp.where(live_new, jnp.exp(score_new - row_max), 0.0)
    denom = jnp.sum(prob_old, axis=1, keepdims=True) + jnp.sum(prob_new, axis=1, keepdims=True)
    weighted = jnp.dot(
        prob_old.astype(jnp.bfloat16), vo_ref[0], preferred_element_type=jnp.float32
    )
    weighted = weighted + jnp.dot(
        prob_new.astype(jnp.bfloat16), values_new, preferred_element_type=jnp.float32
    )
    o_ref[...] = (weighted / denom).astype(o_ref.dtype)


def attention(length, qkv, cosine, sine_signed, k_cache, v_cache):
    new_len = qkv.shape[0]
    cache_rows = k_cache.shape[1]
    heads = qkv.shape[1] // (3 * HD)
    rows = min(128, new_len)
    grid_spec = pltpu.PrefetchScalarGridSpec(
        num_scalar_prefetch=1,
        grid=(heads, new_len // rows),
        in_specs=[
            pl.BlockSpec((rows, HD), lambda h, i, n: (i, 3 * h)),
            pl.BlockSpec((new_len, HD), lambda h, i, n: (0, 3 * h + 1)),
            pl.BlockSpec((new_len, HD), lambda h, i, n: (0, 3 * h + 2)),
            pl.BlockSpec((rows, HD), lambda h, i, n: (i, 0)),
            pl.BlockSpec((rows, HD), lambda h, i, n: (i, 0)),
            pl.BlockSpec((new_len, HD), lambda h, i, n: (0, 0)),
            pl.BlockSpec((new_len, HD), lambda h, i, n: (0, 0)),
            pl.BlockSpec((1, cache_rows, HD), lambda h, i, n: (0, 0, h)),
            pl.BlockSpec((1, cache_rows, HD), lambda h, i, n: (0, 0, h)),
        ],
        out_specs=pl.BlockSpec((rows, HD), lambda h, i, n: (i, h)),
    )
    return pl.pallas_call(
        attention_kernel,
        grid_spec=grid_spec,
        out_shape=jax.ShapeDtypeStruct((new_len, heads * HD), jnp.bfloat16),
        name="cached_attention",
    )(length, qkv, qkv, qkv, cosine, sine_signed, cosine, sine_signed, k_cache, v_cache)


def body(
    tokens,
    cache_len,
    attn_gain,
    w_qkv,
    k_cache,
    v_cache,
    w_out,
    moe_gain,
    w_shared,
    w_shared_down,
    expert_ids,
    expert_weights,
    expert_slot,
    w_expert,
    w_expert_down,
):
    req_local, qrows, width = tokens.shape
    head_count = lax.axis_size("head")
    tok_count = lax.axis_size("tok")
    new_len = qrows * head_count
    head_local = w_out.shape[0] // HD
    cache_rows = k_cache.shape[1]
    normed = normalize(lax.all_gather(tokens, "head", axis=1, tiled=True), attn_gain)
    qkv = jnp.dot(normed[0], w_qkv, preferred_element_type=jnp.float32)
    length = cache_len[0]
    positions = length + jnp.arange(new_len, dtype=jnp.int32)
    half_dim = HD // 2
    freqs = 10000.0 ** (-jnp.arange(half_dim, dtype=jnp.float32) / half_dim)
    angles = positions.astype(jnp.float32)[:, None] * freqs[None, :]
    cosine = jnp.cos(angles)
    sine_part = jnp.sin(angles)
    cosine = jnp.concatenate([cosine, cosine], axis=1)
    sine_signed = jnp.concatenate([-sine_part, sine_part], axis=1)
    outputs = [attention(cache_len, qkv, cosine, sine_signed, k_cache, v_cache)]
    heads_out = jnp.stack(outputs, axis=1)
    row_block = heads_out
    attn_rows = lax.psum_scatter(
        jnp.einsum("crk,kd->crd", row_block, w_out, preferred_element_type=jnp.float32).astype(
            jnp.bfloat16
        ),
        "head",
        scatter_dimension=0,
        tiled=True,
    ).astype(jnp.float32)
    middle = (tokens.astype(jnp.float32) + jnp.transpose(attn_rows, (1, 0, 2))).astype(jnp.bfloat16)
    normed_mid = normalize(middle, moe_gain)
    gate_up = jnp.einsum(
        "rcd,djz->jcrz",
        lax.all_gather(normed_mid, "head", axis=1, tiled=True),
        w_shared,
        preferred_element_type=jnp.float32,
    )
    hidden_rows = (jax.nn.silu(gate_up[0]) * gate_up[1]).astype(jnp.bfloat16)
    row_block = hidden_rows
    shared_rows = lax.psum_scatter(
        jnp.einsum(
            "crz,zd->crd", row_block, w_shared_down, preferred_element_type=jnp.float32
        ).astype(jnp.bfloat16),
        "head",
        scatter_dimension=0,
        tiled=True,
    ).astype(jnp.float32)
    capacity = 2 * qrows * TOP // E
    slots = req_local * capacity
    local_rows = req_local * qrows
    flat_ids = expert_ids.reshape(req_local, qrows * TOP)
    hits = (flat_ids[:, :, None] == jnp.arange(E, dtype=jnp.int32)[None, None, :]).astype(jnp.int32)
    ranks = jnp.sum((jnp.cumsum(hits, axis=1) - 1) * hits, axis=2)
    slot_of = ranks + jnp.arange(req_local, dtype=jnp.int32)[:, None] * capacity
    place_of = jnp.sum(hits * expert_slot[None, None, :], axis=2)
    target = (place_of * slots + slot_of).reshape(local_rows, TOP)
    columns = jnp.arange(E * slots, dtype=jnp.int32)
    matches = (target[:, :, None] == columns[None, None, :]).astype(jnp.float32)
    placement = jnp.sum(matches, axis=1).astype(jnp.bfloat16)
    routing_matrix = jnp.sum(matches * expert_weights.reshape(local_rows, TOP)[:, :, None], axis=1)
    flat_mid = normed_mid.reshape(local_rows, width)
    outgoing = lax.dot_general(
        placement, flat_mid, (((0,), (0,)), ((), ())), preferred_element_type=jnp.float32
    ).astype(jnp.bfloat16)
    devices = head_count * tok_count
    per_device = max(1, E // devices)
    copies = max(1, devices // E)
    outgoing = outgoing.reshape(E, 1, slots, width)
    if copies > 1:
        outgoing = jnp.broadcast_to(outgoing, (E, copies, slots, width))
    outgoing = outgoing.reshape(devices, per_device, slots, width)
    unit_count = w_expert.shape[2] // per_device
    w_down = w_expert_down.reshape(per_device, unit_count, width)
    chunks = CHUNKS if slots % CHUNKS == 0 else 1
    step = slots // chunks
    received = [
        lax.all_to_all(
            outgoing[:, :, c * step : (c + 1) * step],
            ("head", "tok"),
            split_axis=0,
            concat_axis=0,
            tiled=True,
        )
        for c in range(chunks)
    ]
    received[0], shared_rows = lax.optimization_barrier((received[0], shared_rows))
    routing_parts = routing_matrix.reshape(local_rows, E, slots)
    routed = None
    for c in range(chunks):
        expert_parts = []
        for e in range(per_device):
            w_pair = w_expert[:, :, e * unit_count : (e + 1) * unit_count]
            gate_up = jnp.einsum(
                "gsd,dju->jgsu", received[c][:, e], w_pair, preferred_element_type=jnp.float32
            )
            hidden_part = (jax.nn.silu(gate_up[0]) * gate_up[1]).astype(jnp.bfloat16)
            expert_parts.append(
                jnp.einsum(
                    "gsu,ud->gsd", hidden_part, w_down[e], preferred_element_type=jnp.float32
                ).astype(jnp.bfloat16)
            )
        partial_out = jnp.stack(expert_parts, axis=1)
        back = lax.all_to_all(partial_out, ("head", "tok"), split_axis=0, concat_axis=0, tiled=True)
        summed = jnp.sum(back.reshape(E, copies, step, width).astype(jnp.float32), axis=1)
        part = jnp.dot(
            routing_parts[:, :, c * step : (c + 1) * step].reshape(local_rows, E * step),
            summed.reshape(E * step, width),
            precision=lax.Precision.HIGHEST,
            preferred_element_type=jnp.float32,
        )
        routed = part if routed is None else routed + part
    routed = routed.reshape(req_local, qrows, width)
    layer_out = middle.astype(jnp.float32) + jnp.transpose(shared_rows, (1, 0, 2)) + routed
    return layer_out.astype(jnp.bfloat16)


def solution(mesh):
    return jax.shard_map(
        body,
        mesh=mesh,
        in_specs=(
            P("tok", "head", None),
            P("tok"),
            P(),
            P(None, "head"),
            P("tok", None, "head"),
            P("tok", None, "head"),
            P("head", None),
            P(),
            P(None, None, "head"),
            P("head", None),
            P("tok", "head", None),
            P("tok", "head", None),
            P(),
            P(None, None, ("head", "tok")),
            P(("head", "tok"), None),
        ),
        out_specs=P("tok", "head", None),
        check_vma=False,
    )
```

profile of v0, /device:TPU:0, one launch (start us, length us, event | category | flops | bytes accessed | tf_op | source)
XLA Modules:
  0.0 459.3 jit_solution(17106071493156136177)
XLA Ops:
  10.1 24.1 %all-gather.3.cloned.1.call-done = bf16[1,512,2048]{2,1,0:T(8,128)(2,1)} async-done(((bf16[1,128,2048]{2,1,0:T(8,128)(2,1)}), bf16[1,512,2048]{2,1,0:T(8,128)(2,1)}) %all-gather.3.cloned.1.call-update) | async-done | bytes 2097168 | tf_op jit(solution)/shard_map/all_gather | solution.py:159
  36.3 8.5 %fusion.69.q_ref.kn_ref.vn_ref = f32[512,1536]{1,0:T(8,128)} fusion(bf16[2048,1536]{1,0:T(8,128)(2,1)} %param.18, bf16[1,512,2048]{2,1,0:T(8,128)(2,1)} %all-gather.3.cloned.1.call-done, f32[2048]{0:T(1024)S(1)} %copy-done.12, f32[512]{0:T(512)S(1)} %add_rsqrt_fusion), kind=kOutput, calls=%fused_computation.69 | convolution fusion | flops 3225419776 | bytes 11544576 | tf_op jit(solution)/shard_map/dot_general | solution.py:160
  44.9 30.5 %cached_attention.1 = bf16[512,512]{1,0:T(8,128)(2,1)} custom-call(s32[1]{0:T(128)} %copy.165.len_ref, f32[512,1536]{1,0:T(8,128)} %fusion.69.q_ref.kn_ref.vn_ref, f32[512,1536]{1,0:T(8,128)} %fusion.69.q_ref.kn_ref.vn_ref, f32[512,1536]{1,0:T(8,128)} %fusion.69.q_ref.kn_ref.vn_ref, f32[512,128]{1,0:T(8,128)} %get-tuple-element.24.cq_ref.ck_ref, ...), custom_call_target="tpu_custom_call" | custom-call | tf_op jit(solution)/shard_map/cached_attention/pallas_call | solution.py:128
  92.5 18.9 %reduce-scatter.3.cloned.1.call-done = bf16[128,1,2048]{2,0,1:T(8,128)(2,1)} async-done(((bf16[512,1,2048]{2,0,1:T(8,128)(2,1)}), bf16[128,1,2048]{2,0,1:T(8,128)(2,1)}) %reduce-scatter.3.cloned.1.call-update) | async-done | bytes 524304 | tf_op jit(solution)/shard_map/reduce_scatter | solution.py:173
  120.9 4.9 %copy.133 = bf16[32,2,12,2048]{3,1,2,0:T(2,128)(2,1)} copy(bf16[32,2,12,2048]{3,2,1,0:T(8,128)(2,1)S(1)} %get-tuple-element.15) | data formatting | bytes 6291456
  131.3 19.8 %fusion.103 = (bf16[2048,2,1408]{2,1,0:T(2,128)(2,1)}, bf16[2048,2,1408]{2,1,0:T(2,128)(2,1)}) fusion(bf16[2048,2,2816]{2,1,0:T(2,128)(2,1)} %param.28), kind=kLoop, calls=%fused_computation.123 | loop fusion | bytes 46137344 | tf_op jit(solution)/shard_map/slice | solution.py:243
  156.0 47.7 %all-to-all-done.2 = bf16[32,2,12,2048]{3,1,2,0:T(2,128)(2,1)} async-done(((bf16[32,2,12,2048]{3,1,2,0:T(2,128)(2,1)}), bf16[32,2,12,2048]{3,1,2,0:T(2,128)(2,1)}, u32[]{:S(2)}, u32[]{:S(2)}) %all-to-all-start.2) | async-done | bytes 3145760 | tf_op jit(solution)/shard_map/all_to_all | solution.py:228
  207.3 5.9 %fusion.71 = f32[512,2,704]{0,2,1:T(8,128)S(1)} fusion(bf16[2048,2,704]{0,2,1:T(8,128)(2,1)} %param.23, bf16[1,512,2048]{2,1,0:T(8,128)(2,1)} %all-gather.5.cloned.1.call-done), kind=kOutput, calls=%fused_computation.70 | convolution fusion | flops 2952790016 | bytes 10747904 | tf_op jit(solution)/shard_map/rcd,djz->jcrz/dot_general | solution.py:183
  216.6 8.3 %fusion.105 = (bf16[32,1,12,2048]{3,1,2,0:T(2,128)(2,1)S(1)}, bf16[32,1,12,2048]{3,1,2,0:T(2,128)(2,1)S(1)}) fusion(bf16[32,2,12,2048]{3,1,2,0:T(2,128)(2,1)} %all-to-all-done.2), kind=kLoop, calls=%fused_computation.125 | loop fusion | bytes 6291456 | tf_op jit(solution)/shard_map/slice | solution.py:245
  224.8 13.1 %fusion.27 = f32[2,32,12,1408]{3,1,2,0:T(8,128)S(1)} fusion(bf16[2048,2,1408]{2,1,0:T(2,128)(2,1)} %get-tuple-element.14, bf16[32,1,12,2048]{3,1,2,0:T(2,128)(2,1)S(1)} %get-tuple-element.18), kind=kOutput, calls=%fused_computation.32 | convolution fusion | flops 4429185024 | bytes 17432576 | tf_op jit(solution)/shard_map/gsd,dju->jgsu/dot_general | solution.py:244
  237.9 5.5 %fusion.45 = bf16[32,1,12,2048]{3,0,2,1:T(8,128)(2,1)S(1)} fusion(bf16[2816,2048]{1,0:T(8,128)(2,1)} %param.29, f32[2,32,12,1408]{3,1,2,0:T(8,128)S(1)} %fusion.27), kind=kOutput, calls=%fused_computation.44 | convolution fusion | flops 2218622976 | bytes 11665408 | tf_op jit(solution)/shard_map/gsu,ud->gsd/dot_general | solution.py:249
  243.5 6.1 %fusion.28 = f32[2,32,12,1408]{3,1,2,0:T(8,128)S(1)} fusion(bf16[2048,2,1408]{2,1,0:T(2,128)(2,1)S(1)} %bitcast.233, bf16[32,1,12,2048]{3,1,2,0:T(2,128)(2,1)S(1)} %get-tuple-element.17), kind=kOutput, calls=%fused_computation.33 | convolution fusion | flops 4429185024 | bytes 17432576 | tf_op jit(solution)/shard_map/gsd,dju->jgsu/dot_general | solution.py:244
  249.6 5.3 %fusion.51 = bf16[32,1,12,2048]{3,0,2,1:T(8,128)(2,1)S(1)} fusion(bf16[2816,2048]{1,0:T(8,128)(2,1)} %param.29, f32[2,32,12,1408]{3,1,2,0:T(8,128)S(1)} %fusion.28), kind=kOutput, calls=%fused_computation.46 | convolution fusion | flops 2218622976 | bytes 11665408 | tf_op jit(solution)/shard_map/gsu,ud->gsd/dot_general | solution.py:249
  255.2 5.3 %copy.119 = bf16[32,2,12,2048]{3,1,2,0:T(2,128)(2,1)} copy(bf16[32,2,12,2048]{3,0,2,1:T(8,128)(2,1)S(1)} %pad_maximum_fusion.1) | data formatting | bytes 6291456 | tf_op jit(solution)/shard_map/stack | solution.py:253
  262.7 17.6 %all-to-all-done = bf16[32,2,12,2048]{3,1,2,0:T(2,128)(2,1)} async-done(((bf16[32,2,12,2048]{3,1,2,0:T(2,128)(2,1)}), bf16[32,2,12,2048]{3,1,2,0:T(2,128)(2,1)}, u32[]{:S(2)}, u32[]{:S(2)}) %all-to-all-start) | async-done | bytes 3145760 | tf_op jit(solution)/shard_map/all_to_all | solution.py:228
  287.5 10.7 %fusion.26 = f32[2,32,12,1408]{3,1,2,0:T(8,128)S(1)} fusion(bf16[2048,2,1408]{2,1,0:T(2,128)(2,1)} %get-tuple-element.14, bf16[32,2,12,2048]{3,0,2,1:T(8,128)(2,1)S(1)} %copy.106), kind=kOutput, calls=%fused_computation.31 | convolution fusion | flops 4429185024 | bytes 17432576 | tf_op jit(solution)/shard_map/gsd,dju->jgsu/dot_general | solution.py:244
  298.2 5.4 %fusion.48 = bf16[32,1,12,2048]{3,0,2,1:T(8,128)(2,1)S(1)} fusion(bf16[2816,2048]{1,0:T(8,128)(2,1)} %param.29, f32[2,32,12,1408]{3,1,2,0:T(8,128)S(1)} %fusion.26), kind=kOutput, calls=%fused_computation.45 | convolution fusion | flops 2218622976 | bytes 11665408 | tf_op jit(solution)/shard_map/gsu,ud->gsd/dot_general | solution.py:249
  308.3 5.3 %fusion.54 = bf16[32,1,12,2048]{3,0,2,1:T(8,128)(2,1)S(1)} fusion(bf16[2816,2048]{1,0:T(8,128)(2,1)} %param.29, f32[2,32,12,1408]{3,1,0,2:T(8,128)S(1)} %fusion.23), kind=kOutput, calls=%fused_computation.47 | convolution fusion | flops 2218622976 | bytes 11665408 | tf_op jit(solution)/shard_map/gsu,ud->gsd/dot_general | solution.py:249
  318.8 38.1 %all-to-all-done.3 = bf16[32,2,12,2048]{3,1,2,0:T(2,128)(2,1)} async-done(((bf16[32,2,12,2048]{3,1,2,0:T(2,128)(2,1)}), bf16[32,2,12,2048]{3,1,2,0:T(2,128)(2,1)}, u32[]{:S(2)}, u32[]{:S(2)}) %all-to-all-start.3) | async-done | bytes 3145760 | tf_op jit(solution)/shard_map/all_to_all | solution.py:254
  362.6 5.4 %copy.120 = bf16[32,2,12,2048]{3,2,1,0:T(8,128)(2,1)} copy(bf16[32,2,12,2048]{3,1,2,0:T(2,128)(2,1)} %all-to-all-done.3) | data formatting | bytes 6291456 | tf_op jit(solution)/shard_map/all_to_all | solution.py:254
  368.0 6.2 %reshape.312 = bf16[768,2048]{1,0:T(8,128)(2,1)} reshape(bf16[32,2,12,2048]{3,2,1,0:T(8,128)(2,1)} %copy.120) | data formatting | bytes 6291456 | tf_op jit(solution)/shard_map/reshape | solution.py:258
  374.1 59.4 %all-to-all-done.1 = bf16[32,2,12,2048]{3,1,2,0:T(2,128)(2,1)} async-done(((bf16[32,2,12,2048]{3,1,2,0:T(2,128)(2,1)}), bf16[32,2,12,2048]{3,1,2,0:T(2,128)(2,1)}, u32[]{:S(2)}, u32[]{:S(2)}) %all-to-all-start.1) | async-done | bytes 3145760 | tf_op jit(solution)/shard_map/all_to_all | solution.py:254
  433.6 5.4 %copy.113 = bf16[32,2,12,2048]{3,2,1,0:T(8,128)(2,1)} copy(bf16[32,2,12,2048]{3,1,2,0:T(2,128)(2,1)} %all-to-all-done.1) | data formatting | bytes 6291456 | tf_op jit(solution)/shard_map/all_to_all | solution.py:254
  439.0 6.2 %reshape.310 = bf16[768,2048]{1,0:T(8,128)(2,1)} reshape(bf16[32,2,12,2048]{3,2,1,0:T(8,128)(2,1)} %copy.113) | data formatting | bytes 6291456 | tf_op jit(solution)/shard_map/reshape | solution.py:258
  (97 shorter events, 81.0 us)
Async XLA Ops:
  6.5 206.7 %copy-start = (bf16[704,2048]{1,0:T(8,128)(2,1)S(1)}, bf16[704,2048]{1,0:T(8,128)(2,1)}, u32[]{:S(2)}) copy-start(bf16[704,2048]{1,0:T(8,128)(2,1)} %param.24) | copy-start | bytes 8650756
  6.5 29.8 %copy-start.12 = (f32[2048]{0:T(1024)S(1)}, f32[2048]{0:T(1024)}, u32[]{:S(2)}) copy-start(f32[2048]{0:T(1024)} %param.17) | copy-start | bytes 24580
  6.5 27.7 %all-gather.3.cloned.1.call-start = ((), (), s32[]{:S(2)}) async-start(), calls=%async_computation.6 | async-start | bytes 2621440 | tf_op jit(solution)/shard_map/all_gather | solution.py:159
  7.3 104.2 %reduce-scatter.3.cloned.1.call-start = ((), (), s32[]{:S(2)}) async-start(), calls=%async_computation.7 | async-start | bytes 2621440 | tf_op jit(solution)/shard_map/reduce_scatter | solution.py:173
  75.4 4.4 copy-start.9
  79.8 9.3 %copy-start.11 = (s32[64]{0:T(128)S(1)}, s32[64]{0:T(128)}, u32[]{:S(2)}) copy-start(s32[64]{0:T(128)} %param.27) | copy-start | bytes 772
  79.8 10.6 %copy-start.10 = (f32[1,128,6]{1,0,2:T(1,128)S(1)}, f32[1,128,6]{1,0,2:T(1,128)}, u32[]{:S(2)}) copy-start(f32[1,128,6]{1,0,2:T(1,128)} %param.26) | copy-start | bytes 9220
  79.8 31.7 %copy-start.4 = (bf16[1,128,2048]{2,1,0:T(8,128)(2,1)S(1)}, bf16[1,128,2048]{2,1,0:T(8,128)(2,1)}, u32[]{:S(2)}) copy-start(bf16[1,128,2048]{2,1,0:T(8,128)(2,1)} %param.15) | copy-start | bytes 1572868
  79.8 33.0 %copy-start.8 = (f32[2048]{0:T(1024)S(1)}, f32[2048]{0:T(1024)}, u32[]{:S(2)}) copy-start(f32[2048]{0:T(1024)} %param.22) | copy-start | bytes 24580
  125.8 77.9 %all-to-all-start.2 = ((bf16[32,2,12,2048]{3,1,2,0:T(2,128)(2,1)}), bf16[32,2,12,2048]{3,1,2,0:T(2,128)(2,1)}, u32[]{:S(2)}, u32[]{:S(2)}) async-start(bf16[32,2,12,2048]{3,1,2,0:T(2,128)(2,1)} %copy.133), calls=%async_computation.4 | async-start | bytes 6291456 | tf_op jit(solution)/shard_map/all_to_all | solution.py:228
  130.5 76.8 %all-gather.5.cloned.1.call-start = ((), (), s32[]{:S(2)}) async-start(), calls=%async_computation.8 | async-start | bytes 2621440 | tf_op jit(solution)/shard_map/all_gather | solution.py:185
  131.3 19.8 %copy-start.2 = (bf16[32,2,12,2048]{3,2,1,0:T(8,128)(2,1)S(1)}, bf16[32,2,12,2048]{3,2,1,0:T(8,128)(2,1)}, u32[]{:S(2)}) copy-start(bf16[32,2,12,2048]{3,2,1,0:T(8,128)(2,1)} %get-tuple-element.16) | copy-start | bytes 9437188
  203.7 76.6 %all-to-all-start = ((bf16[32,2,12,2048]{3,1,2,0:T(2,128)(2,1)}), bf16[32,2,12,2048]{3,1,2,0:T(2,128)(2,1)}, u32[]{:S(2)}, u32[]{:S(2)}) async-start(bf16[32,2,12,2048]{3,1,2,0:T(2,128)(2,1)} %copy.129), calls=%async_computation.1 | async-start | bytes 6291456 | tf_op jit(solution)/shard_map/all_to_all | solution.py:228
  207.2 53.3 %reduce-scatter.5.cloned.1.call-start = ((), (), s32[]{:S(2)}) async-start(), calls=%async_computation.9 | async-start | bytes 2621440 | tf_op jit(solution)/shard_map/reduce_scatter | solution.py:191
  224.8 18.6 %slice-start = ((s8[11534336]{0:T(1024)(128)(4,1)}), s8[4194304]{0:T(1024)(128)(4,1)S(1)}, s32[]{:S(2)}) async-start(s8[11534336]{0:T(1024)(128)(4,1)} %bitcast.232), calls=%async_computation.10 | async-start | bytes 8388608
  224.8 18.6 %slice-start.1 = ((s8[11534336]{0:T(1024)(128)(4,1)}), s8[4194304]{0:T(1024)(128)(4,1)S(1)}, s32[]{:S(2)}) async-start(s8[11534336]{0:T(1024)(128)(4,1)} %bitcast.232), calls=%async_computation.11 | async-start | bytes 8388608
  237.9 5.5 %slice-start.2 = ((s8[11534336]{0:T(1024)(128)(4,1)}), s8[3145728]{0:T(1024)(128)(4,1)S(1)}, s32[]{:S(2)}) async-start(s8[11534336]{0:T(1024)(128)(4,1)} %bitcast.232), calls=%async_computation.12 | async-start | bytes 6291456
  280.3 76.6 %all-to-all-start.3 = ((bf16[32,2,12,2048]{3,1,2,0:T(2,128)(2,1)}), bf16[32,2,12,2048]{3,1,2,0:T(2,128)(2,1)}, u32[]{:S(2)}, u32[]{:S(2)}) async-start(bf16[32,2,12,2048]{3,1,2,0:T(2,128)(2,1)} %copy.119), calls=%async_computation.5 | async-start | bytes 6291456 | tf_op jit(solution)/shard_map/all_to_all | solution.py:254
  287.5 16.2 %slice-start.3 = ((s8[11534336]{0:T(1024)(128)(4,1)}), s8[4194304]{0:T(1024)(128)(4,1)S(1)}, s32[]{:S(2)}) async-start(s8[11534336]{0:T(1024)(128)(4,1)} %bitcast.234), calls=%async_computation.13 | async-start | bytes 8388608
  287.5 16.2 %slice-start.4 = ((s8[11534336]{0:T(1024)(128)(4,1)}), s8[4194304]{0:T(1024)(128)(4,1)S(1)}, s32[]{:S(2)}) async-start(s8[11534336]{0:T(1024)(128)(4,1)} %bitcast.234), calls=%async_computation.14 | async-start | bytes 8388608
  298.2 5.5 %slice-start.5 = ((s8[11534336]{0:T(1024)(128)(4,1)}), s8[3145728]{0:T(1024)(128)(4,1)S(1)}, s32[]{:S(2)}) async-start(s8[11534336]{0:T(1024)(128)(4,1)} %bitcast.234), calls=%async_computation.15 | async-start | bytes 6291456
  318.8 41.8 %copy-start.6 = (f32[128,1536]{1,0:T(8,128)S(1)}, f32[128,1536]{1,0:T(8,128)}, u32[]{:S(2)}) copy-start(f32[128,1536]{1,0:T(8,128)} %get-tuple-element.10) | copy-start | bytes 2359300
  356.9 76.7 %all-to-all-start.1 = ((bf16[32,2,12,2048]{3,1,2,0:T(2,128)(2,1)}), bf16[32,2,12,2048]{3,1,2,0:T(2,128)(2,1)}, u32[]{:S(2)}, u32[]{:S(2)}) async-start(bf16[32,2,12,2048]{3,1,2,0:T(2,128)(2,1)} %copy.112), calls=%async_computation.3 | async-start | bytes 6291456 | tf_op jit(solution)/shard_map/all_to_all | solution.py:254
  445.2 7.4 %copy-start.1 = (bf16[704,2048]{1,0:T(8,128)(2,1)S(1)}, bf16[704,2048]{1,0:T(8,128)(2,1)}, u32[]{:S(2)}) copy-start(bf16[704,2048]{1,0:T(8,128)(2,1)} %param.24) | copy-start | bytes 8650756
  (3 other events, 11.0 us)
Sparse Core Ops, SparseCore 0:
  8.9 25.2 all-gather.2
  80.0 31.4 reduce-scatter.2
  133.0 37.1 all-gather.4
  216.7 38.9 reduce-scatter.4
where the time goes:
time: 464 us; the launch traced here: 459 us
  waiting for transfers between devices  207 us (45%)
  matrix products  88.5 us (19%)
  local copies, waits for them, and re-layouts  84.2 us (18%)
  Pallas kernels  30.5 us (7%)
  other arithmetic  18.5 us (4%)
  starting transfers between devices  15.6 us (3%)
  between operations  14.5 us (3%)
    all_to_all x2, waiting for transfers between devices, body(): lax.all_to_all(partial_out, ('head', 'tok'), split_axis=0, concat_axis=0,...  97.6 us
    all_to_all x2, waiting for transfers between devices, body(): lax.all_to_all(outgoing[:, :, c * step:(c + 1) * step], ('head', 'tok'),...  65.3 us
    dot_general x4, matrix products, body(): jnp.einsum('gsd,dju->jgsu', received[c][:, e], w_pair, preferred_element_...  34.5 us
    pallas_call x1, Pallas kernels, attention(): pl.pallas_call(attention_kernel, grid_spec=grid_spec, out_shape=jax.Shape...  30.5 us
    all_gather x1, waiting for transfers between devices, body(): lax.all_gather(tokens, 'head', axis=1, tiled=True)  24.1 us
    dot_general x4, matrix products, body(): jnp.einsum('gsu,ud->gsd', hidden_part, w_down[e], preferred_element_type=...  21.5 us
    slice x1, local copies, waits for them, and re-layouts, body(): w_pair = w_expert[:, :, e * unit_count:(e + 1) * unit_count]  19.8 us
    reduce_scatter x1, waiting for transfers between devices, body(): lax.psum_scatter(jnp.einsum('crk,kd->crd', row_block, w_out, preferred_el...  18.9 us
  transfers between devices with their start and end apart: 8, of which 6 were waited for; matrix products, arithmetic and copies ran while one was open for 31% of the time, Pallas kernels for 0%

commit v1 on v0

--- a/solution.py
+++ b/solution.py
@@ -14,7 +14,6 @@
 
 EPS = 1e-06
 NEG_BIG = -1e30
-CHUNKS = 2
 
 
 def normalize(values, gain_vector):
@@ -222,40 +221,28 @@
     outgoing = outgoing.reshape(devices, per_device, slots, width)
     unit_count = w_expert.shape[2] // per_device
     w_down = w_expert_down.reshape(per_device, unit_count, width)
-    chunks = CHUNKS if slots % CHUNKS == 0 else 1
-    step = slots // chunks
+    groups = E // per_device
     received = [
-        lax.all_to_all(
-            outgoing[:, :, c * step : (c + 1) * step],
-            ("head", "tok"),
-            split_axis=0,
-            concat_axis=0,
-            tiled=True,
-        )
-        for c in range(chunks)
+        lax.all_to_all(outgoing[:, c], ("head", "tok"), split_axis=0, concat_axis=0, tiled=True)
+        for c in range(per_device)
     ]
     received[0], shared_rows = lax.optimization_barrier((received[0], shared_rows))
-    routing_parts = routing_matrix.reshape(local_rows, E, slots)
+    routing_parts = routing_matrix.reshape(local_rows, groups, per_device, slots)
     routed = None
-    for c in range(chunks):
-        expert_parts = []
-        for e in range(per_device):
-            w_pair = w_expert[:, :, e * unit_count : (e + 1) * unit_count]
-            gate_up = jnp.einsum(
-                "gsd,dju->jgsu", received[c][:, e], w_pair, preferred_element_type=jnp.float32
-            )
-            hidden_part = (jax.nn.silu(gate_up[0]) * gate_up[1]).astype(jnp.bfloat16)
-            expert_parts.append(
-                jnp.einsum(
-                    "gsu,ud->gsd", hidden_part, w_down[e], preferred_element_type=jnp.float32
-                ).astype(jnp.bfloat16)
-            )
-        partial_out = jnp.stack(expert_parts, axis=1)
-        back = lax.all_to_all(partial_out, ("head", "tok"), split_axis=0, concat_axis=0, tiled=True)
-        summed = jnp.sum(back.reshape(E, copies, step, width).astype(jnp.float32), axis=1)
+    for c in range(per_device):
+        w_pair = w_expert[:, :, c * unit_count : (c + 1) * unit_count]
+        gate_up = jnp.einsum(
+            "gsd,dju->jgsu", received[c], w_pair, preferred_element_type=jnp.float32
+        )
+        hidden_part = (jax.nn.silu(gate_up[0]) * gate_up[1]).astype(jnp.bfloat16)
+        expert_part = jnp.einsum(
+            "gsu,ud->gsd", hidden_part, w_down[c], preferred_element_type=jnp.float32
+        ).astype(jnp.bfloat16)
+        back = lax.all_to_all(expert_part, ("head", "tok"), split_axis=0, concat_axis=0, tiled=True)
+        summed = jnp.sum(back.reshape(groups, copies, slots, width).astype(jnp.float32), axis=1)
         part = jnp.dot(
-            routing_parts[:, :, c * step : (c + 1) * step].reshape(local_rows, E * step),
-            summed.reshape(E * step, width),
+            routing_parts[:, :, c].reshape(local_rows, groups * slots),
+            summed.reshape(groups * slots, width),
             precision=lax.Precision.HIGHEST,
             preferred_element_type=jnp.float32,
         )

time: 464 us -> 454 us (0.978)
  waiting for transfers between devices: 207 us -> 264 us
  local copies, waits for them, and re-layouts: 84.2 us -> 27.5 us
  matrix products: 88.5 us -> 83.3 us
    all_to_all x4, waiting for transfers between devices: 163 us -> 187 us  [the longest x2 116 us: body(): lax.all_to_all(expert_part, ('head', 'tok'), split_axis=0, concat_axis=0,...]
    reduce_scatter x1, waiting for transfers between devices: 0.01 us -> 20.3 us  [body(): lax.psum_scatter(jnp.einsum('crz,zd->crd', row_block, w_shared_down, pref...]
    reshape x4 -> x0, local copies, waits for them, and re-layouts: 13.9 us -> none  [the longest x2 12.3 us: body(): summed.reshape(E * step, width)]
    reduce_scatter x1, waiting for transfers between devices: 18.9 us -> 31.6 us  [body(): lax.psum_scatter(jnp.einsum('crk,kd->crd', row_block, w_out, preferred_el...]
    slice x5 -> x3, local copies, waits for them, and re-layouts: 32.4 us -> 20.9 us  [the longest x1 18.9 us: body(): w_pair = w_expert[:, :, c * unit_count:(c + 1) * unit_count]]
    all_to_all x2 -> x0, local copies, waits for them, and re-layouts: 10.9 us -> none  [body(): lax.all_to_all(partial_out, ('head', 'tok'), split_axis=0, concat_axis=0,...]
    another operation x7 -> x5, local copies, waits for them, and re-layouts: 12.8 us -> 2.7 us  [the longest x2 10.2 us: body(): partial_out = jnp.stack(expert_parts, axis=1)]
    unnamed x42 -> x20, local copies, waits for them, and re-layouts: 10 us -> 0.15 us
  transfers between devices with their start and end apart: 8 -> 8, of which waited for: 6 -> 7; matrix products, arithmetic and copies ran while one was open for 31% -> 23% of each run, Pallas kernels for 0% -> 0%
where the time goes in v1:
time: 454 us; the launch traced here: 452 us
  waiting for transfers between devices  264 us (58%)
  matrix products  83.3 us (18%)
  Pallas kernels  30.3 us (7%)
  local copies, waits for them, and re-layouts  27.5 us (6%)
  other arithmetic  17.8 us (4%)
  starting transfers between devices  15.8 us (3%)
  between operations  14.1 us (3%)
    all_to_all x2, waiting for transfers between devices, body(): lax.all_to_all(expert_part, ('head', 'tok'), split_axis=0, concat_axis=0,...  116 us
    all_to_all x2, waiting for transfers between devices, body(): lax.all_to_all(outgoing[:, c], ('head', 'tok'), split_axis=0, concat_axis...  71 us
    reduce_scatter x1, waiting for transfers between devices, body(): lax.psum_scatter(jnp.einsum('crk,kd->crd', row_block, w_out, preferred_el...  31.6 us
    pallas_call x1, Pallas kernels, attention(): pl.pallas_call(attention_kernel, grid_spec=grid_spec, out_shape=jax.Shape...  30.3 us
    dot_general x2, matrix products, body(): jnp.einsum('gsd,dju->jgsu', received[c], w_pair, preferred_element_type=j...  29.6 us
    all_gather x1, waiting for transfers between devices, body(): lax.all_gather(tokens, 'head', axis=1, tiled=True)  24.1 us
    reduce_scatter x1, waiting for transfers between devices, body(): lax.psum_scatter(jnp.einsum('crz,zd->crd', row_block, w_shared_down, pref...  20.3 us
    dot_general x2, matrix products, body(): jnp.einsum('gsu,ud->gsd', hidden_part, w_down[c], preferred_element_type=...  19.1 us
  transfers between devices with their start and end apart: 8, of which 7 were waited for; matrix products, arithmetic and copies ran while one was open for 23% of the time, Pallas kernels for 0%

profile of v1, /device:TPU:0, one launch (start us, length us, event | category | flops | bytes accessed | tf_op | source)
XLA Modules:
  0.0 452.5 jit_solution(2602892278592979631)
XLA Ops:
  10.1 24.1 %all-gather.3.cloned.1.call-done = bf16[1,512,2048]{2,1,0:T(8,128)(2,1)} async-done(((bf16[1,128,2048]{2,1,0:T(8,128)(2,1)}), bf16[1,512,2048]{2,1,0:T(8,128)(2,1)}) %all-gather.3.cloned.1.call-update) | async-done | bytes 2097168 | tf_op jit(solution)/shard_map/all_gather | solution.py:158
  36.3 8.5 %fusion.33.q_ref.kn_ref.vn_ref = f32[512,1536]{1,0:T(8,128)} fusion(bf16[2048,1536]{1,0:T(8,128)(2,1)} %param.18, bf16[1,512,2048]{2,1,0:T(8,128)(2,1)} %all-gather.3.cloned.1.call-done, f32[2048]{0:T(1024)S(1)} %copy-done.8, f32[512]{0:T(512)S(1)} %add_rsqrt_fusion), kind=kOutput, calls=%fused_computation.42 | convolution fusion | flops 3225419776 | bytes 11544576 | tf_op jit(solution)/shard_map/dot_general | solution.py:159
  44.9 30.3 %cached_attention.1 = bf16[512,512]{1,0:T(8,128)(2,1)} custom-call(s32[1]{0:T(128)} %copy.75.len_ref, f32[512,1536]{1,0:T(8,128)} %fusion.33.q_ref.kn_ref.vn_ref, f32[512,1536]{1,0:T(8,128)} %fusion.33.q_ref.kn_ref.vn_ref, f32[512,1536]{1,0:T(8,128)} %fusion.33.q_ref.kn_ref.vn_ref, f32[512,128]{1,0:T(8,128)} %get-tuple-element.22.cq_ref.ck_ref, ...), custom_call_target="tpu_custom_call" | custom-call | tf_op jit(solution)/shard_map/cached_attention/pallas_call | solution.py:127
  75.1 4.4 fusion.23
  79.6 31.6 %reduce-scatter.3.cloned.1.call-done = bf16[128,1,2048]{2,0,1:T(8,128)(2,1)} async-done(((bf16[512,1,2048]{2,0,1:T(8,128)(2,1)}), bf16[128,1,2048]{2,0,1:T(8,128)(2,1)}) %reduce-scatter.3.cloned.1.call-update) | async-done | bytes 524304 | tf_op jit(solution)/shard_map/reduce_scatter | solution.py:172
  115.6 4.4 reduce-window.6
  133.2 4.7 %all-to-all-start = ((bf16[32,24,2048]{2,1,0:T(8,128)(2,1)}), bf16[32,24,2048]{2,1,0:T(8,128)(2,1)}, u32[]{:S(2)}, u32[]{:S(2)}) async-start(bf16[32,24,2048]{2,1,0:T(8,128)(2,1)} %get-tuple-element.16), calls=%async_computation.1 | async-start | bytes 6291456 | tf_op jit(solution)/shard_map/all_to_all | solution.py:226
  138.2 5.9 %fusion.35 = f32[512,2,704]{0,2,1:T(8,128)S(1)} fusion(bf16[2048,2,704]{0,2,1:T(8,128)(2,1)} %param.23, bf16[1,512,2048]{2,1,0:T(8,128)(2,1)} %all-gather.5.cloned.1.call-done), kind=kOutput, calls=%fused_computation.43 | convolution fusion | flops 2952790016 | bytes 10747904 | tf_op jit(solution)/shard_map/rcd,djz->jcrz/dot_general | solution.py:182
  144.1 3.3 fusion.24
  147.4 18.9 %fusion.57 = (bf16[2048,2,1408]{2,1,0:T(2,128)(2,1)}, bf16[2048,2,1408]{2,1,0:T(2,128)(2,1)}) fusion(bf16[2048,2,2816]{2,1,0:T(2,128)(2,1)} %param.28), kind=kLoop, calls=%fused_computation.86 | loop fusion | bytes 46137344 | tf_op jit(solution)/shard_map/slice | solution.py:233
  166.3 20.3 %reduce-scatter.5.cloned.1.call-done = bf16[128,1,2048]{2,0,1:T(8,128)(2,1)} async-done(((bf16[512,1,2048]{2,0,1:T(8,128)(2,1)}), bf16[128,1,2048]{2,0,1:T(8,128)(2,1)}) %reduce-scatter.5.cloned.1.call-update) | async-done | bytes 524304 | tf_op jit(solution)/shard_map/reduce_scatter | solution.py:190
  188.8 22.2 %all-to-all-done = bf16[32,24,2048]{2,1,0:T(8,128)(2,1)} async-done(((bf16[32,24,2048]{2,1,0:T(8,128)(2,1)}), bf16[32,24,2048]{2,1,0:T(8,128)(2,1)}, u32[]{:S(2)}, u32[]{:S(2)}) %all-to-all-start) | async-done | bytes 3145760 | tf_op jit(solution)/shard_map/all_to_all | solution.py:226
  211.0 3.5 all-to-all-start.2
  214.5 14.8 %fusion.8 = f32[2,32,24,1408]{3,2,0,1:T(8,128)S(1)} fusion(bf16[2048,2,1408]{2,1,0:T(2,128)(2,1)} %get-tuple-element.14, bf16[32,24,2048]{2,1,0:T(8,128)(2,1)} %all-to-all-done), kind=kOutput, calls=%fused_computation.11 | convolution fusion | flops 8858370048 | bytes 23330816 | tf_op jit(solution)/shard_map/gsd,dju->jgsu/dot_general | solution.py:234
  229.3 9.5 %fusion.15 = bf16[32,24,2048]{2,1,0:T(8,128)(2,1)} fusion(bf16[2816,2048]{1,0:T(8,128)(2,1)} %param.29, f32[2,32,24,1408]{3,2,0,1:T(8,128)S(1)} %fusion.8), kind=kOutput, calls=%fused_computation.25 | convolution fusion | flops 4437245952 | bytes 17563648 | tf_op jit(solution)/shard_map/gsu,ud->gsd/dot_general | solution.py:238
  238.8 48.8 %all-to-all-done.2 = bf16[32,24,2048]{2,1,0:T(8,128)(2,1)} async-done(((bf16[32,24,2048]{2,1,0:T(8,128)(2,1)}), bf16[32,24,2048]{2,1,0:T(8,128)(2,1)}, u32[]{:S(2)}, u32[]{:S(2)}) %all-to-all-start.2) | async-done | bytes 3145760 | tf_op jit(solution)/shard_map/all_to_all | solution.py:226
  287.6 3.8 all-to-all-start.1
  291.4 14.8 %fusion.9 = f32[2,32,24,1408]{3,2,0,1:T(8,128)S(1)} fusion(bf16[2048,2,1408]{2,1,0:T(2,128)(2,1)} %get-tuple-element.13, bf16[32,24,2048]{2,1,0:T(8,128)(2,1)} %all-to-all-done.2), kind=kOutput, calls=%fused_computation.12 | convolution fusion | flops 8858370048 | bytes 23330816 | tf_op jit(solution)/shard_map/gsd,dju->jgsu/dot_general | solution.py:234
  306.1 9.5 %fusion.18 = bf16[32,24,2048]{2,1,0:T(8,128)(2,1)} fusion(bf16[2816,2048]{1,0:T(8,128)(2,1)} %param.29, f32[2,32,24,1408]{3,2,0,1:T(8,128)S(1)} %fusion.9), kind=kOutput, calls=%fused_computation.26 | convolution fusion | flops 4437245952 | bytes 17563648 | tf_op jit(solution)/shard_map/gsu,ud->gsd/dot_general | solution.py:238
  315.7 48.5 %all-to-all-done.1 = bf16[32,24,2048]{2,1,0:T(8,128)(2,1)} async-done(((bf16[32,24,2048]{2,1,0:T(8,128)(2,1)}), bf16[32,24,2048]{2,1,0:T(8,128)(2,1)}, u32[]{:S(2)}, u32[]{:S(2)}) %all-to-all-start.1) | async-done | bytes 3145760 | tf_op jit(solution)/shard_map/all_to_all | solution.py:241
  364.2 3.5 all-to-all-start.3
  368.8 4.5 %fusion.60 = f32[128,2048]{1,0:T(8,128)} fusion(f32[128,768]{0,1:T(8,128)S(1)} %bitcast.151, bf16[768,2048]{1,0:T(8,128)(2,1)} %bitcast.30), kind=kOutput, calls=%fused_computation.89 | convolution fusion | flops 2415919104 | bytes 4587520 | tf_op jit(solution)/shard_map/dot_general | solution.py:243
  373.4 67.5 %all-to-all-done.3 = bf16[32,24,2048]{2,1,0:T(8,128)(2,1)} async-done(((bf16[32,24,2048]{2,1,0:T(8,128)(2,1)}), bf16[32,24,2048]{2,1,0:T(8,128)(2,1)}, u32[]{:S(2)}, u32[]{:S(2)}) %all-to-all-start.3) | async-done | bytes 3145760 | tf_op jit(solution)/shard_map/all_to_all | solution.py:241
  440.8 5.1 %fusion.27 = bf16[1,128,2048]{2,1,0:T(8,128)(2,1)} fusion(f32[128,2048]{1,0:T(8,128)} %fusion.60, f32[128,768]{0,1:T(8,128)} %bitcast.150, bf16[768,2048]{1,0:T(8,128)(2,1)} %bitcast.39, f32[128,1,2048]{2,0,1:T(8,128)} %convert_element_type.104, bf16[128,1,2048]{2,0,1:T(8,128)(2,1)} %reduce-scatter.3.cloned.1.call-done, bf16[1,128,2048]{2,1,0:T(8,128)(2,1)S(1)} %copy-done.2), kind=kOutput, calls=%fused_computation.38 | convolution fusion | flops 2418278400 | bytes 7208960 | tf_op jit(solution)/shard_map/dot_general | solution.py:243
  (57 shorter events, 26.0 us)
Async XLA Ops:
  6.5 137.5 %copy-start = (bf16[704,2048]{1,0:T(8,128)(2,1)S(1)}, bf16[704,2048]{1,0:T(8,128)(2,1)}, u32[]{:S(2)}) copy-start(bf16[704,2048]{1,0:T(8,128)(2,1)} %param.24) | copy-start | bytes 8650756
  6.5 29.8 %copy-start.8 = (f32[2048]{0:T(1024)S(1)}, f32[2048]{0:T(1024)}, u32[]{:S(2)}) copy-start(f32[2048]{0:T(1024)} %param.17) | copy-start | bytes 24580
  6.5 27.7 %all-gather.3.cloned.1.call-start = ((), (), s32[]{:S(2)}) async-start(), calls=%async_computation.6 | async-start | bytes 2621440 | tf_op jit(solution)/shard_map/all_gather | solution.py:158
  7.3 103.9 %reduce-scatter.3.cloned.1.call-start = ((), (), s32[]{:S(2)}) async-start(), calls=%async_computation.7 | async-start | bytes 2621440 | tf_op jit(solution)/shard_map/reduce_scatter | solution.py:172
  75.1 36.1 %copy-start.2 = (bf16[1,128,2048]{2,1,0:T(8,128)(2,1)S(1)}, bf16[1,128,2048]{2,1,0:T(8,128)(2,1)}, u32[]{:S(2)}) copy-start(bf16[1,128,2048]{2,1,0:T(8,128)(2,1)} %param.15) | copy-start | bytes 1572868
  75.1 37.4 %copy-start.4 = (f32[2048]{0:T(1024)S(1)}, f32[2048]{0:T(1024)}, u32[]{:S(2)}) copy-start(f32[2048]{0:T(1024)} %param.22) | copy-start | bytes 24580
  79.5 35.0 %copy-start.6 = (f32[1,128,6]{1,0,2:T(1,128)S(1)}, f32[1,128,6]{1,0,2:T(1,128)}, u32[]{:S(2)}) copy-start(f32[1,128,6]{1,0,2:T(1,128)} %param.26) | copy-start | bytes 9220
  79.5 35.1 %copy-start.5 = (s32[1,128,6]{1,0,2:T(1,128)S(1)}, s32[1,128,6]{1,0,2:T(1,128)}, u32[]{:S(2)}) copy-start(s32[1,128,6]{1,0,2:T(1,128)} %param.25) | copy-start | bytes 9220
  79.5 44.3 %copy-start.7 = (s32[64]{0:T(128)S(1)}, s32[64]{0:T(128)}, u32[]{:S(2)}) copy-start(s32[64]{0:T(128)} %param.27) | copy-start | bytes 772
  79.6 58.6 %all-gather.5.cloned.1.call-start = ((), (), s32[]{:S(2)}) async-start(), calls=%async_computation.8 | async-start | bytes 2621440 | tf_op jit(solution)/shard_map/all_gather | solution.py:184
  133.2 77.7 %all-to-all-start = ((bf16[32,24,2048]{2,1,0:T(8,128)(2,1)}), bf16[32,24,2048]{2,1,0:T(8,128)(2,1)}, u32[]{:S(2)}, u32[]{:S(2)}) async-start(bf16[32,24,2048]{2,1,0:T(8,128)(2,1)} %get-tuple-element.16), calls=%async_computation.1 | async-start | bytes 6291456 | tf_op jit(solution)/shard_map/all_to_all | solution.py:226
  137.9 48.7 %reduce-scatter.5.cloned.1.call-start = ((), (), s32[]{:S(2)}) async-start(), calls=%async_computation.9 | async-start | bytes 2621440 | tf_op jit(solution)/shard_map/reduce_scatter | solution.py:190
  211.0 76.6 %all-to-all-start.2 = ((bf16[32,24,2048]{2,1,0:T(8,128)(2,1)}), bf16[32,24,2048]{2,1,0:T(8,128)(2,1)}, u32[]{:S(2)}, u32[]{:S(2)}) async-start(bf16[32,24,2048]{2,1,0:T(8,128)(2,1)} %get-tuple-element.15), calls=%async_computation.4 | async-start | bytes 6291456 | tf_op jit(solution)/shard_map/all_to_all | solution.py:226
  287.6 76.6 %all-to-all-start.1 = ((bf16[32,24,2048]{2,1,0:T(8,128)(2,1)}), bf16[32,24,2048]{2,1,0:T(8,128)(2,1)}, u32[]{:S(2)}, u32[]{:S(2)}) async-start(bf16[32,24,2048]{2,1,0:T(8,128)(2,1)} %fusion.15), calls=%async_computation.3 | async-start | bytes 6291456 | tf_op jit(solution)/shard_map/all_to_all | solution.py:241
  315.7 52.1 %copy-start.3 = (f32[128,1536]{1,0:T(8,128)S(1)}, f32[128,1536]{1,0:T(8,128)}, u32[]{:S(2)}) copy-start(f32[128,1536]{1,0:T(8,128)} %get-tuple-element.10) | copy-start | bytes 2359300
  364.2 76.6 %all-to-all-start.3 = ((bf16[32,24,2048]{2,1,0:T(8,128)(2,1)}), bf16[32,24,2048]{2,1,0:T(8,128)(2,1)}, u32[]{:S(2)}, u32[]{:S(2)}) async-start(bf16[32,24,2048]{2,1,0:T(8,128)(2,1)} %fusion.18), calls=%async_computation.5 | async-start | bytes 6291456 | tf_op jit(solution)/shard_map/all_to_all | solution.py:241
  368.8 77.1 %copy-start.1 = (bf16[704,2048]{1,0:T(8,128)(2,1)S(1)}, bf16[704,2048]{1,0:T(8,128)(2,1)}, u32[]{:S(2)}) copy-start(bf16[704,2048]{1,0:T(8,128)(2,1)} %param.24) | copy-start | bytes 8650756
Sparse Core Ops, SparseCore 0:
  8.9 25.2 all-gather.2
  79.7 31.4 reduce-scatter.2
  114.7 22.5 all-gather.4
  147.5 39.0 reduce-scatter.4

commit v2 on v1

--- a/solution.py
+++ b/solution.py
@@ -155,7 +155,24 @@
     new_len = qrows * head_count
     head_local = w_out.shape[0] // HD
     cache_rows = k_cache.shape[1]
-    normed = normalize(lax.all_gather(tokens, "head", axis=1, tiled=True), attn_gain)
+    capacity = 2 * qrows * TOP // E
+    slots = req_local * capacity
+    local_rows = req_local * qrows
+    flat_ids = expert_ids.reshape(req_local, qrows * TOP)
+    hits = (flat_ids[:, :, None] == jnp.arange(E, dtype=jnp.int32)[None, None, :]).astype(jnp.int32)
+    ranks = jnp.sum((jnp.cumsum(hits, axis=1) - 1) * hits, axis=2)
+    slot_of = ranks + jnp.arange(req_local, dtype=jnp.int32)[:, None] * capacity
+    place_of = jnp.sum(hits * expert_slot[None, None, :], axis=2)
+    target = (place_of * slots + slot_of).reshape(local_rows, TOP)
+    columns = jnp.arange(E * slots, dtype=jnp.int32)
+    matches = (target[:, :, None] == columns[None, None, :]).astype(jnp.float32)
+    placement = jnp.sum(matches, axis=1).astype(jnp.bfloat16)
+    routing_matrix = jnp.sum(matches * expert_weights.reshape(local_rows, TOP)[:, :, None], axis=1)
+    gathered = lax.all_gather(tokens, "head", axis=1, tiled=True)
+    gathered, placement, routing_matrix = lax.optimization_barrier(
+        (gathered, placement, routing_matrix)
+    )
+    normed = normalize(gathered, attn_gain)
     qkv = jnp.dot(normed[0], w_qkv, preferred_element_type=jnp.float32)
     length = cache_len[0]
     positions = length + jnp.arange(new_len, dtype=jnp.int32)
@@ -195,19 +212,6 @@
         scatter_dimension=0,
         tiled=True,
     ).astype(jnp.float32)
-    capacity = 2 * qrows * TOP // E
-    slots = req_local * capacity
-    local_rows = req_local * qrows
-    flat_ids = expert_ids.reshape(req_local, qrows * TOP)
-    hits = (flat_ids[:, :, None] == jnp.arange(E, dtype=jnp.int32)[None, None, :]).astype(jnp.int32)
-    ranks = jnp.sum((jnp.cumsum(hits, axis=1) - 1) * hits, axis=2)
-    slot_of = ranks + jnp.arange(req_local, dtype=jnp.int32)[:, None] * capacity
-    place_of = jnp.sum(hits * expert_slot[None, None, :], axis=2)
-    target = (place_of * slots + slot_of).reshape(local_rows, TOP)
-    columns = jnp.arange(E * slots, dtype=jnp.int32)
-    matches = (target[:, :, None] == columns[None, None, :]).astype(jnp.float32)
-    placement = jnp.sum(matches, axis=1).astype(jnp.bfloat16)
-    routing_matrix = jnp.sum(matches * expert_weights.reshape(local_rows, TOP)[:, :, None], axis=1)
     flat_mid = normed_mid.reshape(local_rows, width)
     outgoing = lax.dot_general(
         placement, flat_mid, (((0,), (0,)), ((), ())), preferred_element_type=jnp.float32

time: 454 us -> 451 us (level)
    all_gather x1, waiting for transfers between devices: 0.02 us -> 31.8 us  [body(): lax.all_gather(normed_mid, 'head', axis=1, tiled=True)]
    all_to_all x2, waiting for transfers between devices: 71 us -> 48.8 us  [body(): lax.all_to_all(outgoing[:, c], ('head', 'tok'), split_axis=0, concat_axis...]
    all_gather x1, waiting for transfers between devices: 24.1 us -> 17.1 us  [body(): gathered = lax.all_gather(tokens, 'head', axis=1, tiled=True)]
  transfers between devices with their start and end apart: 8 -> 8, of which waited for: 7 -> 7; matrix products, arithmetic and copies ran while one was open for 23% -> 22% of each run, Pallas kernels for 0% -> 0%
where the time goes in v2:
time: 451 us; the launch traced here: 450 us
  waiting for transfers between devices  267 us (59%)
  matrix products  83.4 us (18%)
  Pallas kernels  30.3 us (7%)
  local copies, waits for them, and re-layouts  25.7 us (6%)
  starting transfers between devices  15.8 us (4%)
  other arithmetic  14.3 us (3%)
  between operations  14 us (3%)
    all_to_all x2, waiting for transfers between devices, body(): lax.all_to_all(expert_part, ('head', 'tok'), split_axis=0, concat_axis=0,...  116 us
    all_to_all x2, waiting for transfers between devices, body(): lax.all_to_all(outgoing[:, c], ('head', 'tok'), split_axis=0, concat_axis...  48.8 us
    all_gather x1, waiting for transfers between devices, body(): lax.all_gather(normed_mid, 'head', axis=1, tiled=True)  31.8 us
    reduce_scatter x1, waiting for transfers between devices, body(): lax.psum_scatter(jnp.einsum('crk,kd->crd', row_block, w_out, preferred_el...  31.5 us
    pallas_call x1, Pallas kernels, attention(): pl.pallas_call(attention_kernel, grid_spec=grid_spec, out_shape=jax.Shape...  30.3 us
    dot_general x2, matrix products, body(): jnp.einsum('gsd,dju->jgsu', received[c], w_pair, preferred_element_type=j...  29.6 us
    reduce_scatter x1, waiting for transfers between devices, body(): lax.psum_scatter(jnp.einsum('crz,zd->crd', row_block, w_shared_down, pref...  20.9 us
    dot_general x2, matrix products, body(): jnp.einsum('gsu,ud->gsd', hidden_part, w_down[c], preferred_element_type=...  19.1 us
  transfers between devices with their start and end apart: 8, of which 7 were waited for; matrix products, arithmetic and copies ran while one was open for 22% of the time, Pallas kernels for 0%

profile of v2, /device:TPU:0, one launch (start us, length us, event | category | flops | bytes accessed | tf_op | source)
XLA Modules:
  0.0 450.2 jit_solution(1970832725082937094)
XLA Ops:
  17.2 17.1 %all-gather.3.cloned.1.call-done = bf16[1,512,2048]{2,1,0:T(8,128)(2,1)} async-done(((bf16[1,128,2048]{2,1,0:T(8,128)(2,1)}), bf16[1,512,2048]{2,1,0:T(8,128)(2,1)}) %all-gather.3.cloned.1.call-update) | async-done | bytes 2097168 | tf_op jit(solution)/shard_map/all_gather | solution.py:171
  36.4 8.5 %fusion.33.q_ref.kn_ref.vn_ref = f32[512,1536]{1,0:T(8,128)} fusion(bf16[2048,1536]{1,0:T(8,128)(2,1)} %param.18, bf16[1,512,2048]{2,1,0:T(8,128)(2,1)} %all-gather.3.cloned.1.call-done, f32[2048]{0:T(1024)S(1)} %copy-done.5, f32[512]{0:T(512)S(1)} %add_rsqrt_fusion), kind=kOutput, calls=%fused_computation.42 | convolution fusion | flops 3225419776 | bytes 11544576 | tf_op jit(solution)/shard_map/dot_general | solution.py:176
  44.9 30.3 %cached_attention.1 = bf16[512,512]{1,0:T(8,128)(2,1)} custom-call(s32[1]{0:T(128)} %copy.75.len_ref, f32[512,1536]{1,0:T(8,128)} %fusion.33.q_ref.kn_ref.vn_ref, f32[512,1536]{1,0:T(8,128)} %fusion.33.q_ref.kn_ref.vn_ref, f32[512,1536]{1,0:T(8,128)} %fusion.33.q_ref.kn_ref.vn_ref, f32[512,128]{1,0:T(8,128)} %get-tuple-element.28.cq_ref.ck_ref, ...), custom_call_target="tpu_custom_call" | custom-call | tf_op jit(solution)/shard_map/cached_attention/pallas_call | solution.py:127
  75.2 4.4 fusion.23
  79.7 31.5 %reduce-scatter.3.cloned.1.call-done = bf16[128,1,2048]{2,0,1:T(8,128)(2,1)} async-done(((bf16[512,1,2048]{2,0,1:T(8,128)(2,1)}), bf16[128,1,2048]{2,0,1:T(8,128)(2,1)}) %reduce-scatter.3.cloned.1.call-update) | async-done | bytes 524304 | tf_op jit(solution)/shard_map/reduce_scatter | solution.py:189
  117.5 3.3 slice_bitcast_fusion
  120.8 4.7 %all-to-all-start = ((bf16[32,24,2048]{2,1,0:T(8,128)(2,1)}), bf16[32,24,2048]{2,1,0:T(8,128)(2,1)}, u32[]{:S(2)}, u32[]{:S(2)}) async-start(bf16[32,24,2048]{2,1,0:T(8,128)(2,1)} %get-tuple-element.22), calls=%async_computation.1 | async-start | bytes 6291456 | tf_op jit(solution)/shard_map/all_to_all | solution.py:230
  125.8 31.8 %all-gather.5.cloned.1.call-done = bf16[1,512,2048]{2,1,0:T(8,128)(2,1)} async-done(((bf16[1,128,2048]{2,1,0:T(8,128)(2,1)}), bf16[1,512,2048]{2,1,0:T(8,128)(2,1)}) %all-gather.5.cloned.1.call-update) | async-done | bytes 2097168 | tf_op jit(solution)/shard_map/all_gather | solution.py:201
  157.6 5.9 %fusion.35 = f32[512,2,704]{0,2,1:T(8,128)S(1)} fusion(bf16[2048,2,704]{0,2,1:T(8,128)(2,1)} %param.23, bf16[1,512,2048]{2,1,0:T(8,128)(2,1)} %all-gather.5.cloned.1.call-done), kind=kOutput, calls=%fused_computation.43 | convolution fusion | flops 2952790016 | bytes 10747904 | tf_op jit(solution)/shard_map/rcd,djz->jcrz/dot_general | solution.py:199
  163.5 3.3 fusion.24
  166.8 18.9 %fusion.56 = (bf16[2048,2,1408]{2,1,0:T(2,128)(2,1)}, bf16[2048,2,1408]{2,1,0:T(2,128)(2,1)}) fusion(bf16[2048,2,2816]{2,1,0:T(2,128)(2,1)} %param.28), kind=kLoop, calls=%fused_computation.85 | loop fusion | bytes 46137344 | tf_op jit(solution)/shard_map/slice | solution.py:237
  185.7 20.9 %reduce-scatter.5.cloned.1.call-done = bf16[128,1,2048]{2,0,1:T(8,128)(2,1)} async-done(((bf16[512,1,2048]{2,0,1:T(8,128)(2,1)}), bf16[128,1,2048]{2,0,1:T(8,128)(2,1)}) %reduce-scatter.5.cloned.1.call-update) | async-done | bytes 524304 | tf_op jit(solution)/shard_map/reduce_scatter | solution.py:207
  208.7 3.5 all-to-all-start.2
  212.3 14.8 %fusion.8 = f32[2,32,24,1408]{3,2,0,1:T(8,128)S(1)} fusion(bf16[2048,2,1408]{2,1,0:T(2,128)(2,1)} %get-tuple-element.20, bf16[32,24,2048]{2,1,0:T(8,128)(2,1)} %all-to-all-done), kind=kOutput, calls=%fused_computation.11 | convolution fusion | flops 8858370048 | bytes 23330816 | tf_op jit(solution)/shard_map/gsd,dju->jgsu/dot_general | solution.py:238
  227.1 9.5 %fusion.15 = bf16[32,24,2048]{2,1,0:T(8,128)(2,1)} fusion(bf16[2816,2048]{1,0:T(8,128)(2,1)} %param.29, f32[2,32,24,1408]{3,2,0,1:T(8,128)S(1)} %fusion.8), kind=kOutput, calls=%fused_computation.25 | convolution fusion | flops 4437245952 | bytes 17563648 | tf_op jit(solution)/shard_map/gsu,ud->gsd/dot_general | solution.py:242
  236.6 48.8 %all-to-all-done.2 = bf16[32,24,2048]{2,1,0:T(8,128)(2,1)} async-done(((bf16[32,24,2048]{2,1,0:T(8,128)(2,1)}), bf16[32,24,2048]{2,1,0:T(8,128)(2,1)}, u32[]{:S(2)}, u32[]{:S(2)}) %all-to-all-start.2) | async-done | bytes 3145760 | tf_op jit(solution)/shard_map/all_to_all | solution.py:230
  285.4 3.8 all-to-all-start.1
  289.1 14.8 %fusion.9 = f32[2,32,24,1408]{3,2,0,1:T(8,128)S(1)} fusion(bf16[2048,2,1408]{2,1,0:T(2,128)(2,1)} %get-tuple-element.19, bf16[32,24,2048]{2,1,0:T(8,128)(2,1)} %all-to-all-done.2), kind=kOutput, calls=%fused_computation.12 | convolution fusion | flops 8858370048 | bytes 23330816 | tf_op jit(solution)/shard_map/gsd,dju->jgsu/dot_general | solution.py:238
  303.9 9.6 %fusion.18 = bf16[32,24,2048]{2,1,0:T(8,128)(2,1)} fusion(bf16[2816,2048]{1,0:T(8,128)(2,1)} %param.29, f32[2,32,24,1408]{3,2,0,1:T(8,128)S(1)} %fusion.9), kind=kOutput, calls=%fused_computation.26 | convolution fusion | flops 4437245952 | bytes 17563648 | tf_op jit(solution)/shard_map/gsu,ud->gsd/dot_general | solution.py:242
  313.5 48.5 %all-to-all-done.1 = bf16[32,24,2048]{2,1,0:T(8,128)(2,1)} async-done(((bf16[32,24,2048]{2,1,0:T(8,128)(2,1)}), bf16[32,24,2048]{2,1,0:T(8,128)(2,1)}, u32[]{:S(2)}, u32[]{:S(2)}) %all-to-all-start.1) | async-done | bytes 3145760 | tf_op jit(solution)/shard_map/all_to_all | solution.py:245
  362.0 3.5 all-to-all-start.3
  366.6 4.5 %fusion.59 = f32[128,2048]{1,0:T(8,128)} fusion(f32[128,768]{0,1:T(8,128)S(1)} %bitcast.151, bf16[768,2048]{1,0:T(8,128)(2,1)} %bitcast.30), kind=kOutput, calls=%fused_computation.88 | convolution fusion | flops 2415919104 | bytes 4587520 | tf_op jit(solution)/shard_map/dot_general | solution.py:247
  371.1 67.5 %all-to-all-done.3 = bf16[32,24,2048]{2,1,0:T(8,128)(2,1)} async-done(((bf16[32,24,2048]{2,1,0:T(8,128)(2,1)}), bf16[32,24,2048]{2,1,0:T(8,128)(2,1)}, u32[]{:S(2)}, u32[]{:S(2)}) %all-to-all-start.3) | async-done | bytes 3145760 | tf_op jit(solution)/shard_map/all_to_all | solution.py:245
  438.6 5.1 %fusion.27 = bf16[1,128,2048]{2,1,0:T(8,128)(2,1)} fusion(f32[128,2048]{1,0:T(8,128)} %fusion.59, f32[128,768]{0,1:T(8,128)} %bitcast.150, bf16[768,2048]{1,0:T(8,128)(2,1)} %bitcast.39, f32[128,1,2048]{2,0,1:T(8,128)} %convert_element_type.104, bf16[128,1,2048]{2,0,1:T(8,128)(2,1)} %reduce-scatter.3.cloned.1.call-done, bf16[1,128,2048]{2,1,0:T(8,128)(2,1)S(1)} %copy-done.2), kind=kOutput, calls=%fused_computation.38 | convolution fusion | flops 2418278400 | bytes 7208960 | tf_op jit(solution)/shard_map/dot_general | solution.py:247
  (51 shorter events, 21.9 us)
Async XLA Ops:
  6.5 156.9 %copy-start = (bf16[704,2048]{1,0:T(8,128)(2,1)S(1)}, bf16[704,2048]{1,0:T(8,128)(2,1)}, u32[]{:S(2)}) copy-start(bf16[704,2048]{1,0:T(8,128)(2,1)} %param.24) | copy-start | bytes 8650756
  6.5 29.8 %copy-start.5 = (f32[2048]{0:T(1024)S(1)}, f32[2048]{0:T(1024)}, u32[]{:S(2)}) copy-start(f32[2048]{0:T(1024)} %param.17) | copy-start | bytes 24580
  6.5 27.7 %all-gather.3.cloned.1.call-start = ((), (), s32[]{:S(2)}) async-start(), calls=%async_computation.6 | async-start | bytes 2621440 | tf_op jit(solution)/shard_map/all_gather | solution.py:171
  7.3 103.9 %reduce-scatter.3.cloned.1.call-start = ((), (), s32[]{:S(2)}) async-start(), calls=%async_computation.7 | async-start | bytes 2621440 | tf_op jit(solution)/shard_map/reduce_scatter | solution.py:189
  75.2 36.0 %copy-start.2 = (bf16[1,128,2048]{2,1,0:T(8,128)(2,1)S(1)}, bf16[1,128,2048]{2,1,0:T(8,128)(2,1)}, u32[]{:S(2)}) copy-start(bf16[1,128,2048]{2,1,0:T(8,128)(2,1)} %param.15) | copy-start | bytes 1572868
  75.2 37.3 %copy-start.4 = (f32[2048]{0:T(1024)S(1)}, f32[2048]{0:T(1024)}, u32[]{:S(2)}) copy-start(f32[2048]{0:T(1024)} %param.22) | copy-start | bytes 24580
  79.6 78.0 %all-gather.5.cloned.1.call-start = ((), (), s32[]{:S(2)}) async-start(), calls=%async_computation.8 | async-start | bytes 2621440 | tf_op jit(solution)/shard_map/all_gather | solution.py:201
  120.8 87.9 %all-to-all-start = ((bf16[32,24,2048]{2,1,0:T(8,128)(2,1)}), bf16[32,24,2048]{2,1,0:T(8,128)(2,1)}, u32[]{:S(2)}, u32[]{:S(2)}) async-start(bf16[32,24,2048]{2,1,0:T(8,128)(2,1)} %get-tuple-element.22), calls=%async_computation.1 | async-start | bytes 6291456 | tf_op jit(solution)/shard_map/all_to_all | solution.py:230
  125.5 81.1 %reduce-scatter.5.cloned.1.call-start = ((), (), s32[]{:S(2)}) async-start(), calls=%async_computation.9 | async-start | bytes 2621440 | tf_op jit(solution)/shard_map/reduce_scatter | solution.py:207
  208.7 76.6 %all-to-all-start.2 = ((bf16[32,24,2048]{2,1,0:T(8,128)(2,1)}), bf16[32,24,2048]{2,1,0:T(8,128)(2,1)}, u32[]{:S(2)}, u32[]{:S(2)}) async-start(bf16[32,24,2048]{2,1,0:T(8,128)(2,1)} %get-tuple-element.21), calls=%async_computation.4 | async-start | bytes 6291456 | tf_op jit(solution)/shard_map/all_to_all | solution.py:230
  285.4 76.6 %all-to-all-start.1 = ((bf16[32,24,2048]{2,1,0:T(8,128)(2,1)}), bf16[32,24,2048]{2,1,0:T(8,128)(2,1)}, u32[]{:S(2)}, u32[]{:S(2)}) async-start(bf16[32,24,2048]{2,1,0:T(8,128)(2,1)} %fusion.15), calls=%async_computation.3 | async-start | bytes 6291456 | tf_op jit(solution)/shard_map/all_to_all | solution.py:245
  313.5 52.1 %copy-start.3 = (f32[128,1536]{1,0:T(8,128)S(1)}, f32[128,1536]{1,0:T(8,128)}, u32[]{:S(2)}) copy-start(f32[128,1536]{1,0:T(8,128)} %get-tuple-element.13) | copy-start | bytes 2359300
  362.0 76.6 %all-to-all-start.3 = ((bf16[32,24,2048]{2,1,0:T(8,128)(2,1)}), bf16[32,24,2048]{2,1,0:T(8,128)(2,1)}, u32[]{:S(2)}, u32[]{:S(2)}) async-start(bf16[32,24,2048]{2,1,0:T(8,128)(2,1)} %fusion.18), calls=%async_computation.5 | async-start | bytes 6291456 | tf_op jit(solution)/shard_map/all_to_all | solution.py:245
  366.6 77.1 %copy-start.1 = (bf16[704,2048]{1,0:T(8,128)(2,1)S(1)}, bf16[704,2048]{1,0:T(8,128)(2,1)}, u32[]{:S(2)}) copy-start(bf16[704,2048]{1,0:T(8,128)(2,1)} %param.24) | copy-start | bytes 8650756
Sparse Core Ops, SparseCore 0:
  8.9 25.3 all-gather.2
  79.8 31.3 reduce-scatter.2
  114.7 42.8 all-gather.4
  166.9 39.6 reduce-scatter.4

commit v3 on v2

--- a/solution.py
+++ b/solution.py
@@ -130,6 +130,46 @@
         out_shape=jax.ShapeDtypeStruct((new_len, heads * HD), jnp.bfloat16),
         name="cached_attention",
     )(length, qkv, qkv, qkv, cosine, sine_signed, cosine, sine_signed, k_cache, v_cache)
+
+
+def cross_perm(count, step):
+    pairs = count // 2
+    return [(j, ((j // 2 + step) % pairs) * 2 + j % 2) for j in range(count)]
+
+
+def head_gather(block):
+    count = lax.axis_size("head")
+    pairs = count // 2
+    index = lax.axis_index("head")
+    pair, core = index // 2, index % 2
+    pieces = [block] + [
+        lax.ppermute(block, "head", cross_perm(count, step)) for step in range(1, pairs)
+    ]
+    stacked = jnp.stack(pieces)
+    order = (pair - jnp.arange(pairs, dtype=jnp.int32)) % pairs
+    mine = jnp.take(stacked, order, axis=0)
+    partner = lax.ppermute(mine, "head", [(j, j ^ 1) for j in range(count)])
+    first = jnp.where(core == 0, mine, partner)
+    second = jnp.where(core == 0, partner, mine)
+    return jnp.stack([first, second], axis=1).reshape((count * block.shape[0],) + block.shape[1:])
+
+
+def head_scatter_sum(partial):
+    count = lax.axis_size("head")
+    pairs = count // 2
+    index = lax.axis_index("head")
+    pair, core = index // 2, index % 2
+    blocks = partial.reshape((pairs, 2, partial.shape[0] // count) + partial.shape[1:])
+    mine = jnp.where(core == 0, blocks[:, 0], blocks[:, 1])
+    other = jnp.where(core == 0, blocks[:, 1], blocks[:, 0])
+    received = lax.ppermute(other, "head", [(j, j ^ 1) for j in range(count)])
+    chip_sum = mine.astype(jnp.float32) + received.astype(jnp.float32)
+    result = jnp.take(chip_sum, pair, axis=0)
+    for step in range(1, pairs):
+        outgoing = jnp.take(chip_sum, (pair + step) % pairs, axis=0).astype(jnp.bfloat16)
+        arrived = lax.ppermute(outgoing, "head", cross_perm(count, step))
+        result = result + arrived.astype(jnp.float32)
+    return result
 
 
 def body(
@@ -168,7 +208,7 @@
     matches = (target[:, :, None] == columns[None, None, :]).astype(jnp.float32)
     placement = jnp.sum(matches, axis=1).astype(jnp.bfloat16)
     routing_matrix = jnp.sum(matches * expert_weights.reshape(local_rows, TOP)[:, :, None], axis=1)
-    gathered = lax.all_gather(tokens, "head", axis=1, tiled=True)
+    gathered = head_gather(tokens[0])[None]
     gathered, placement, routing_matrix = lax.optimization_barrier(
         (gathered, placement, routing_matrix)
     )
@@ -184,34 +224,23 @@
     cosine = jnp.concatenate([cosine, cosine], axis=1)
     sine_signed = jnp.concatenate([-sine_part, sine_part], axis=1)
     outputs = [attention(cache_len, qkv, cosine, sine_signed, k_cache, v_cache)]
-    heads_out = jnp.stack(outputs, axis=1)
-    row_block = heads_out
-    attn_rows = lax.psum_scatter(
-        jnp.einsum("crk,kd->crd", row_block, w_out, preferred_element_type=jnp.float32).astype(
-            jnp.bfloat16
-        ),
-        "head",
-        scatter_dimension=0,
-        tiled=True,
-    ).astype(jnp.float32)
-    middle = (tokens.astype(jnp.float32) + jnp.transpose(attn_rows, (1, 0, 2))).astype(jnp.bfloat16)
+    attn_rows = head_scatter_sum(
+        jnp.dot(outputs[0], w_out, preferred_element_type=jnp.float32).astype(jnp.bfloat16)
+    )[None]
+    middle = (tokens.astype(jnp.float32) + attn_rows).astype(jnp.bfloat16)
     normed_mid = normalize(middle, moe_gain)
     gate_up = jnp.einsum(
-        "rcd,djz->jcrz",
-        lax.all_gather(normed_mid, "head", axis=1, tiled=True),
+        "cd,djz->jcz",
+        head_gather(normed_mid[0]),
         w_shared,
         preferred_element_type=jnp.float32,
     )
     hidden_rows = (jax.nn.silu(gate_up[0]) * gate_up[1]).astype(jnp.bfloat16)
-    row_block = hidden_rows
-    shared_rows = lax.psum_scatter(
-        jnp.einsum(
-            "crz,zd->crd", row_block, w_shared_down, preferred_element_type=jnp.float32
-        ).astype(jnp.bfloat16),
-        "head",
-        scatter_dimension=0,
-        tiled=True,
-    ).astype(jnp.float32)
+    shared_rows = head_scatter_sum(
+        jnp.dot(hidden_rows, w_shared_down, preferred_element_type=jnp.float32).astype(
+            jnp.bfloat16
+        )
+    )[None]
     flat_mid = normed_mid.reshape(local_rows, width)
     outgoing = lax.dot_general(
         placement, flat_mid, (((0,), (0,)), ((), ())), preferred_element_type=jnp.float32
@@ -252,7 +281,7 @@
         )
         routed = part if routed is None else routed + part
     routed = routed.reshape(req_local, qrows, width)
-    layer_out = middle.astype(jnp.float32) + jnp.transpose(shared_rows, (1, 0, 2)) + routed
+    layer_out = middle.astype(jnp.float32) + shared_rows + routed
     return layer_out.astype(jnp.bfloat16)
 
 

time: 451 us -> 453 us (level); the launches traced: 450 us -> 446 us
  waiting for transfers between devices: 267 us -> 247 us
  local copies, waits for them, and re-layouts: 25.7 us -> 38.5 us
  between operations: 14 us -> 1.58 us
  other arithmetic: 14.3 us -> 26.4 us
  starting transfers between devices: 15.8 us -> 26.7 us
  matrix products: 83.4 us -> 74.5 us
    reduce_scatter x2 -> x0, waiting for transfers between devices: 52.4 us -> none  [the longest x1 31.5 us: body(): lax.psum_scatter(jnp.einsum('crk,kd->crd', row_block, w_out, preferred_el...]
    ppermute x0 -> x8, waiting for transfers between devices: none -> 49 us  [the longest x2 28.2 us: head_scatter_sum(): arrived = lax.ppermute(outgoing, 'head', cross_perm(count, step))]
    all_gather x2 -> x0, waiting for transfers between devices: 48.9 us -> none  [the longest x1 31.8 us: body(): lax.all_gather(normed_mid, 'head', axis=1, tiled=True)]
    all_to_all x2, waiting for transfers between devices: 48.8 us -> 82.2 us  [body(): lax.all_to_all(outgoing[:, c], ('head', 'tok'), split_axis=0, concat_axis...]
    ppermute x0 -> x8, starting transfers between devices: none -> 9.49 us  [the longest x2 4.74 us: head_gather(): lax.ppermute(block, 'head', cross_perm(count, step))]
    unnamed x14 -> x34, local copies, waits for them, and re-layouts: 1.63 us -> 8.55 us
    select_n x0 -> x5, other arithmetic: none -> 5.96 us  [the longest x3 3.75 us: head_gather(): mine = jnp.take(stacked, order, axis=0)]
    gather x0 -> x2, local copies, waits for them, and re-layouts: none -> 5.63 us  [head_gather(): mine = jnp.take(stacked, order, axis=0)]
  transfers between devices with their start and end apart: 8 -> 12, of which waited for: 7 -> 9; matrix products, arithmetic and copies ran while one was open for 22% -> 21% of each run, Pallas kernels for 0% -> 0%
where the time goes in v3:
time: 453 us; the launch traced here: 446 us
  waiting for transfers between devices  247 us (55%)
  matrix products  74.5 us (16%)
  local copies, waits for them, and re-layouts  38.5 us (8%)
  Pallas kernels  30.4 us (7%)
  starting transfers between devices  26.7 us (6%)
  other arithmetic  26.4 us (6%)
    all_to_all x2, waiting for transfers between devices, body(): lax.all_to_all(expert_part, ('head', 'tok'), split_axis=0, concat_axis=0,...  116 us
    all_to_all x2, waiting for transfers between devices, body(): lax.all_to_all(outgoing[:, c], ('head', 'tok'), split_axis=0, concat_axis...  82.2 us
    pallas_call x1, Pallas kernels, attention(): pl.pallas_call(attention_kernel, grid_spec=grid_spec, out_shape=jax.Shape...  30.4 us
    dot_general x2, matrix products, body(): jnp.einsum('gsd,dju->jgsu', received[c], w_pair, preferred_element_type=j...  29.6 us
    ppermute x2, waiting for transfers between devices, head_scatter_sum(): arrived = lax.ppermute(outgoing, 'head', cross_perm(count, step))  28.2 us
    dot_general x2, matrix products, body(): jnp.einsum('gsu,ud->gsd', hidden_part, w_down[c], preferred_element_type=...  19.2 us
    slice x1, local copies, waits for them, and re-layouts, body(): w_pair = w_expert[:, :, c * unit_count:(c + 1) * unit_count]  18.8 us
    ppermute x2, waiting for transfers between devices, head_gather(): lax.ppermute(block, 'head', cross_perm(count, step))  18.2 us
  transfers between devices with their start and end apart: 12, of which 9 were waited for; matrix products, arithmetic and copies ran while one was open for 21% of the time, Pallas kernels for 0%

profile of v3, /device:TPU:0, one launch (start us, length us, event | category | flops | bytes accessed | tf_op | source)
XLA Modules:
  0.0 445.6 jit_solution(16873393086443092548)
XLA Ops:
  8.5 6.7 %collective-permute-done = bf16[128,2048]{1,0:T(8,128)(2,1)} collective-permute-done((bf16[128,2048]{1,0:T(8,128)(2,1)}, bf16[128,2048]{1,0:T(8,128)(2,1)}, u32[]{:S(2)}, u32[]{:S(2)}) %collective-permute-start) | collective-permute-done | bytes 524320 | tf_op jit(solution)/shard_map/ppermute | solution.py:146
  30.4 5.1 %fusion.31.q_ref.kn_ref.vn_ref = f32[512,1536]{1,0:T(8,128)} fusion(bf16[2048,1536]{1,0:T(8,128)(2,1)S(1)} %bitcast.213, bf16[1,512,2048]{2,1,0:T(8,128)(2,1)S(1)} %bitcast.203, f32[2048]{0:T(1024)S(1)} %copy-done.11, f32[512]{0:T(512)S(1)} %add_rsqrt_fusion), kind=kOutput, calls=%fused_computation.42 | convolution fusion | flops 3225419776 | bytes 11544576 | tf_op jit(solution)/shard_map/dot_general | solution.py:216
  35.5 30.4 %cached_attention.1 = bf16[512,512]{1,0:T(8,128)(2,1)} custom-call(s32[1]{0:T(128)} %copy.98.len_ref, f32[512,1536]{1,0:T(8,128)} %fusion.31.q_ref.kn_ref.vn_ref, f32[512,1536]{1,0:T(8,128)} %fusion.31.q_ref.kn_ref.vn_ref, f32[512,1536]{1,0:T(8,128)} %fusion.31.q_ref.kn_ref.vn_ref, f32[512,128]{1,0:T(8,128)} %get-tuple-element.47.cq_ref.ck_ref, ...), custom_call_target="tpu_custom_call" | custom-call | tf_op jit(solution)/shard_map/cached_attention/pallas_call | solution.py:127
  80.2 12.6 %collective-permute-done.3 = bf16[128,2048]{1,0:T(8,128)(2,1)} collective-permute-done((bf16[128,2048]{1,0:T(8,128)(2,1)S(1)}, bf16[128,2048]{1,0:T(8,128)(2,1)}, u32[]{:S(2)}, u32[]{:S(2)}) %collective-permute-start.3) | collective-permute-done | bytes 524320 | tf_op jit(solution)/shard_map/ppermute | solution.py:170
  96.9 11.5 %collective-permute-done.4 = bf16[128,2048]{1,0:T(8,128)(2,1)S(1)} collective-permute-done((bf16[128,2048]{1,0:T(8,128)(2,1)S(1)}, bf16[128,2048]{1,0:T(8,128)(2,1)S(1)}, u32[]{:S(2)}, u32[]{:S(2)}) %collective-permute-start.4) | collective-permute-done | bytes 524320 | tf_op jit(solution)/shard_map/ppermute | solution.py:146
  113.7 3.0 convolution_convert_fusion
  119.5 3.2 convolution_bitcast_fusion
  127.5 3.2 slice_bitcast_fusion
  130.7 6.4 %all-to-all-start = ((bf16[32,24,2048]{2,1,0:T(8,128)(2,1)}), bf16[32,24,2048]{2,1,0:T(8,128)(2,1)}, u32[]{:S(2)}, u32[]{:S(2)}) async-start(bf16[32,24,2048]{2,1,0:T(8,128)(2,1)} %get-tuple-element.37), calls=%async_computation | async-start | bytes 6291456 | tf_op jit(solution)/shard_map/all_to_all | solution.py:259
  140.9 18.8 %fusion.55 = (bf16[2048,2,1408]{2,1,0:T(2,128)(2,1)}, bf16[2048,2,1408]{2,1,0:T(2,128)(2,1)}) fusion(bf16[2048,2,2816]{2,1,0:T(2,128)(2,1)} %param.32), kind=kLoop, calls=%fused_computation.114 | loop fusion | bytes 46137344 | tf_op jit(solution)/shard_map/slice | solution.py:266
  159.7 15.7 %collective-permute-done.7 = bf16[128,2048]{1,0:T(8,128)(2,1)S(1)} collective-permute-done((bf16[128,2048]{1,0:T(8,128)(2,1)S(1)}, bf16[128,2048]{1,0:T(8,128)(2,1)S(1)}, u32[]{:S(2)}, u32[]{:S(2)}) %collective-permute-start.7) | collective-permute-done | bytes 524320 | tf_op jit(solution)/shard_map/ppermute | solution.py:170
  176.6 33.5 %all-to-all-done = bf16[32,24,2048]{2,1,0:T(8,128)(2,1)} async-done(((bf16[32,24,2048]{2,1,0:T(8,128)(2,1)}), bf16[32,24,2048]{2,1,0:T(8,128)(2,1)}, u32[]{:S(2)}, u32[]{:S(2)}) %all-to-all-start) | async-done | bytes 3145760 | tf_op jit(solution)/shard_map/all_to_all | solution.py:259
  210.1 3.5 all-to-all-start.2
  213.6 14.8 %fusion.8 = f32[2,32,24,1408]{3,2,0,1:T(8,128)S(1)} fusion(bf16[2048,2,1408]{2,1,0:T(2,128)(2,1)} %get-tuple-element.35, bf16[32,24,2048]{2,1,0:T(8,128)(2,1)} %all-to-all-done), kind=kOutput, calls=%fused_computation.13 | convolution fusion | flops 8858370048 | bytes 23330816 | tf_op jit(solution)/shard_map/gsd,dju->jgsu/dot_general | solution.py:267
  228.4 9.6 %fusion.15 = bf16[32,24,2048]{2,1,0:T(8,128)(2,1)} fusion(bf16[2816,2048]{1,0:T(8,128)(2,1)} %param.33, f32[2,32,24,1408]{3,2,0,1:T(8,128)S(1)} %fusion.8), kind=kOutput, calls=%fused_computation.27 | convolution fusion | flops 4437245952 | bytes 17563648 | tf_op jit(solution)/shard_map/gsu,ud->gsd/dot_general | solution.py:271
  238.0 48.7 %all-to-all-done.2 = bf16[32,24,2048]{2,1,0:T(8,128)(2,1)} async-done(((bf16[32,24,2048]{2,1,0:T(8,128)(2,1)}), bf16[32,24,2048]{2,1,0:T(8,128)(2,1)}, u32[]{:S(2)}, u32[]{:S(2)}) %all-to-all-start.2) | async-done | bytes 3145760 | tf_op jit(solution)/shard_map/all_to_all | solution.py:259
  286.7 3.8 all-to-all-start.1
  290.5 14.8 %fusion.9 = f32[2,32,24,1408]{3,2,0,1:T(8,128)S(1)} fusion(bf16[2048,2,1408]{2,1,0:T(2,128)(2,1)} %get-tuple-element.34, bf16[32,24,2048]{2,1,0:T(8,128)(2,1)} %all-to-all-done.2), kind=kOutput, calls=%fused_computation.14 | convolution fusion | flops 8858370048 | bytes 23330816 | tf_op jit(solution)/shard_map/gsd,dju->jgsu/dot_general | solution.py:267
  305.3 9.6 %fusion.18 = bf16[32,24,2048]{2,1,0:T(8,128)(2,1)} fusion(bf16[2816,2048]{1,0:T(8,128)(2,1)} %param.33, f32[2,32,24,1408]{3,2,0,1:T(8,128)S(1)} %fusion.9), kind=kOutput, calls=%fused_computation.28 | convolution fusion | flops 4437245952 | bytes 17563648 | tf_op jit(solution)/shard_map/gsu,ud->gsd/dot_general | solution.py:271
  314.9 48.6 %all-to-all-done.1 = bf16[32,24,2048]{2,1,0:T(8,128)(2,1)} async-done(((bf16[32,24,2048]{2,1,0:T(8,128)(2,1)}), bf16[32,24,2048]{2,1,0:T(8,128)(2,1)}, u32[]{:S(2)}, u32[]{:S(2)}) %all-to-all-start.1) | async-done | bytes 3145760 | tf_op jit(solution)/shard_map/all_to_all | solution.py:274
  363.4 3.5 all-to-all-start.3
  368.1 4.4 fusion.58
  372.4 67.6 %all-to-all-done.3 = bf16[32,24,2048]{2,1,0:T(8,128)(2,1)} async-done(((bf16[32,24,2048]{2,1,0:T(8,128)(2,1)}), bf16[32,24,2048]{2,1,0:T(8,128)(2,1)}, u32[]{:S(2)}, u32[]{:S(2)}) %all-to-all-start.3) | async-done | bytes 3145760 | tf_op jit(solution)/shard_map/all_to_all | solution.py:274
  440.1 5.1 %fusion.25 = bf16[1,128,2048]{2,1,0:T(8,128)(2,1)} fusion(f32[128,2048]{1,0:T(8,128)} %fusion.58, f32[128,768]{0,1:T(8,128)} %bitcast.207, bf16[768,2048]{1,0:T(8,128)(2,1)} %bitcast.50, f32[1,128,2048]{2,1,0:T(8,128)} %fusion.40, bf16[1,128,2048]{2,1,0:T(8,128)(2,1)S(1)} %get-tuple-element.33), kind=kOutput, calls=%fused_computation.38 | convolution fusion | flops 2417229824 | bytes 6684672 | tf_op jit(solution)/shard_map/dot_general | solution.py:276
  (99 shorter events, 60.0 us)
Async XLA Ops:
  0.0 122.7 %copy-start = (bf16[704,2048]{1,0:T(8,128)(2,1)S(1)}, bf16[704,2048]{1,0:T(8,128)(2,1)}, u32[]{:S(2)}) copy-start(bf16[704,2048]{1,0:T(8,128)(2,1)} %param.28) | copy-start | bytes 8650756
  0.0 15.2 %collective-permute-start = (bf16[128,2048]{1,0:T(8,128)(2,1)}, bf16[128,2048]{1,0:T(8,128)(2,1)}, u32[]{:S(2)}, u32[]{:S(2)}) collective-permute-start(bf16[128,2048]{1,0:T(8,128)(2,1)} %bitcast.206), channel_id=1, source_target_pairs={{0,16},{8,24},{16,0},{24,8},{1,17},{9,25},{17,1},{25,9},{2,18},{10... | collective-permute-start | bytes 1572872 | tf_op jit(solution)/shard_map/ppermute | solution.py:146
  22.6 4.3 collective-permute-start.1
  22.8 4.1 copy-start.2
  27.0 2.6 slice-start
  28.6 1.8 slice-start.1
  71.5 3.1 collective-permute-start.2
  78.3 16.3 %copy-start.10 = (f32[2048]{0:T(1024)S(1)}, f32[2048]{0:T(1024)}, u32[]{:S(2)}) copy-start(f32[2048]{0:T(1024)} %param.26) | copy-start | bytes 24580
  78.4 14.4 %collective-permute-start.3 = (bf16[128,2048]{1,0:T(8,128)(2,1)S(1)}, bf16[128,2048]{1,0:T(8,128)(2,1)}, u32[]{:S(2)}, u32[]{:S(2)}) collective-permute-start(bf16[128,2048]{1,0:T(8,128)(2,1)S(1)} %bitcast_convert_fusion.1), channel_id=1, source_target_pairs={{0,16},{8,24},{16,0},{24,8},{1,17},{9,25},{17,1},{25,9},{2,18},{10... | collective-permute-start | bytes 1572872 | tf_op jit(solution)/shard_map/ppermute | solution.py:170
  94.8 13.5 %collective-permute-start.4 = (bf16[128,2048]{1,0:T(8,128)(2,1)S(1)}, bf16[128,2048]{1,0:T(8,128)(2,1)S(1)}, u32[]{:S(2)}, u32[]{:S(2)}) collective-permute-start(bf16[128,2048]{1,0:T(8,128)(2,1)S(1)} %fusion.71), channel_id=1, source_target_pairs={{0,16},{8,24},{16,0},{24,8},{1,17},{9,25},{17,1},{25,9},{2,18},{10... | collective-permute-start | bytes 1572872 | tf_op jit(solution)/shard_map/ppermute | solution.py:146
  96.8 11.5 %copy-start.8 = (bf16[1,128,2048]{2,1,0:T(8,128)(2,1)}, bf16[1,128,2048]{2,1,0:T(8,128)(2,1)S(1)}, u32[]{:S(2)}) copy-start(bf16[1,128,2048]{2,1,0:T(8,128)(2,1)S(1)} %fusion.39) | copy-start | bytes 1572868
  113.6 3.2 copy-start.3
  113.6 3.1 collective-permute-start.5
  116.8 2.2 slice-start.2
  117.0 2.5 slice-start.3
  127.1 10.0 %collective-permute-start.6 = (bf16[2,128,2048]{2,1,0:T(8,128)(2,1)}, bf16[2,128,2048]{2,1,0:T(8,128)(2,1)}, u32[]{:S(2)}, u32[]{:S(2)}) collective-permute-start(bf16[2,128,2048]{2,1,0:T(8,128)(2,1)} %select_bitcast_fusion), channel_id=1, source_target_pairs={{0,8},{8,0},{16,24},{24,16},{1,9},{9,1},{17,25},{25,17},{2,10},{10... | collective-permute-start | bytes 3145736 | tf_op jit(solution)/shard_map/ppermute | solution.py:165
  130.7 6.4 %copy-start.6 = (bf16[512,2048]{1,0:T(8,128)(2,1)S(1)}, bf16[512,2048]{1,0:T(8,128)(2,1)}, u32[]{:S(2)}) copy-start(bf16[512,2048]{1,0:T(8,128)(2,1)} %copy-done.5) | copy-start | bytes 6291460
  130.7 79.4 %all-to-all-start = ((bf16[32,24,2048]{2,1,0:T(8,128)(2,1)}), bf16[32,24,2048]{2,1,0:T(8,128)(2,1)}, u32[]{:S(2)}, u32[]{:S(2)}) async-start(bf16[32,24,2048]{2,1,0:T(8,128)(2,1)} %get-tuple-element.37), calls=%async_computation | async-start | bytes 6291456 | tf_op jit(solution)/shard_map/all_to_all | solution.py:259
  138.9 36.5 %collective-permute-start.7 = (bf16[128,2048]{1,0:T(8,128)(2,1)S(1)}, bf16[128,2048]{1,0:T(8,128)(2,1)S(1)}, u32[]{:S(2)}, u32[]{:S(2)}) collective-permute-start(bf16[128,2048]{1,0:T(8,128)(2,1)S(1)} %bitcast_convert_fusion), channel_id=1, source_target_pairs={{0,16},{8,24},{16,0},{24,8},{1,17},{9,25},{17,1},{25,9},{2,18},{10... | collective-permute-start | bytes 1572872 | tf_op jit(solution)/shard_map/ppermute | solution.py:170
  210.1 76.6 %all-to-all-start.2 = ((bf16[32,24,2048]{2,1,0:T(8,128)(2,1)}), bf16[32,24,2048]{2,1,0:T(8,128)(2,1)}, u32[]{:S(2)}, u32[]{:S(2)}) async-start(bf16[32,24,2048]{2,1,0:T(8,128)(2,1)} %get-tuple-element.36), calls=%async_computation.2 | async-start | bytes 6291456 | tf_op jit(solution)/shard_map/all_to_all | solution.py:259
  286.7 76.8 %all-to-all-start.1 = ((bf16[32,24,2048]{2,1,0:T(8,128)(2,1)}), bf16[32,24,2048]{2,1,0:T(8,128)(2,1)}, u32[]{:S(2)}, u32[]{:S(2)}) async-start(bf16[32,24,2048]{2,1,0:T(8,128)(2,1)} %fusion.15), calls=%async_computation.1 | async-start | bytes 6291456 | tf_op jit(solution)/shard_map/all_to_all | solution.py:274
  314.9 52.1 %copy-start.9 = (f32[128,1536]{1,0:T(8,128)S(1)}, f32[128,1536]{1,0:T(8,128)}, u32[]{:S(2)}) copy-start(f32[128,1536]{1,0:T(8,128)} %get-tuple-element.15) | copy-start | bytes 2359300
  363.4 76.6 %all-to-all-start.3 = ((bf16[32,24,2048]{2,1,0:T(8,128)(2,1)}), bf16[32,24,2048]{2,1,0:T(8,128)(2,1)}, u32[]{:S(2)}, u32[]{:S(2)}) async-start(bf16[32,24,2048]{2,1,0:T(8,128)(2,1)} %fusion.18), calls=%async_computation.3 | async-start | bytes 6291456 | tf_op jit(solution)/shard_map/all_to_all | solution.py:274
  440.1 5.1 %copy-start.1 = (bf16[704,2048]{1,0:T(8,128)(2,1)S(1)}, bf16[704,2048]{1,0:T(8,128)(2,1)}, u32[]{:S(2)}) copy-start(bf16[704,2048]{1,0:T(8,128)(2,1)} %param.28) | copy-start | bytes 8650756
  (4 other events, 5.7 us)

commit v4 on v3

--- a/solution.py
+++ b/solution.py
@@ -229,18 +229,6 @@
     )[None]
     middle = (tokens.astype(jnp.float32) + attn_rows).astype(jnp.bfloat16)
     normed_mid = normalize(middle, moe_gain)
-    gate_up = jnp.einsum(
-        "cd,djz->jcz",
-        head_gather(normed_mid[0]),
-        w_shared,
-        preferred_element_type=jnp.float32,
-    )
-    hidden_rows = (jax.nn.silu(gate_up[0]) * gate_up[1]).astype(jnp.bfloat16)
-    shared_rows = head_scatter_sum(
-        jnp.dot(hidden_rows, w_shared_down, preferred_element_type=jnp.float32).astype(
-            jnp.bfloat16
-        )
-    )[None]
     flat_mid = normed_mid.reshape(local_rows, width)
     outgoing = lax.dot_general(
         placement, flat_mid, (((0,), (0,)), ((), ())), preferred_element_type=jnp.float32
@@ -259,7 +247,6 @@
         lax.all_to_all(outgoing[:, c], ("head", "tok"), split_axis=0, concat_axis=0, tiled=True)
         for c in range(per_device)
     ]
-    received[0], shared_rows = lax.optimization_barrier((received[0], shared_rows))
     routing_parts = routing_matrix.reshape(local_rows, groups, per_device, slots)
     routed = None
     for c in range(per_device):
@@ -271,6 +258,8 @@
         expert_part = jnp.einsum(
             "gsu,ud->gsd", hidden_part, w_down[c], preferred_element_type=jnp.float32
         ).astype(jnp.bfloat16)
+        if c == per_device - 1:
+            expert_part, shared_in = lax.optimization_barrier((expert_part, normed_mid))
         back = lax.all_to_all(expert_part, ("head", "tok"), split_axis=0, concat_axis=0, tiled=True)
         summed = jnp.sum(back.reshape(groups, copies, slots, width).astype(jnp.float32), axis=1)
         part = jnp.dot(
@@ -281,6 +270,18 @@
         )
         routed = part if routed is None else routed + part
     routed = routed.reshape(req_local, qrows, width)
+    gate_up = jnp.einsum(
+        "cd,djz->jcz",
+        head_gather(shared_in[0]),
+        w_shared,
+        preferred_element_type=jnp.float32,
+    )
+    hidden_rows = (jax.nn.silu(gate_up[0]) * gate_up[1]).astype(jnp.bfloat16)
+    shared_rows = head_scatter_sum(
+        jnp.dot(hidden_rows, w_shared_down, preferred_element_type=jnp.float32).astype(
+            jnp.bfloat16
+        )
+    )[None]
     layer_out = middle.astype(jnp.float32) + shared_rows + routed
     return layer_out.astype(jnp.bfloat16)
 

time: 453 us -> 431 us (0.951); the launches traced: 446 us -> 429 us
  waiting for transfers between devices: 247 us -> 214 us
  starting transfers between devices: 26.7 us -> 36.8 us
    all_to_all x2, waiting for transfers between devices: 116 us -> 67.5 us  [body(): lax.all_to_all(expert_part, ('head', 'tok'), split_axis=0, concat_axis=0,...]
    all_to_all x2, waiting for transfers between devices: 82.2 us -> 103 us  [body(): lax.all_to_all(outgoing[:, c], ('head', 'tok'), split_axis=0, concat_axis...]
    ppermute x2, waiting for transfers between devices: 28.2 us -> 12.8 us  [head_scatter_sum(): arrived = lax.ppermute(outgoing, 'head', cross_perm(count, step))]
    all_to_all x2, starting transfers between devices: 7.32 us -> 18.4 us  [body(): lax.all_to_all(expert_part, ('head', 'tok'), split_axis=0, concat_axis=0,...]
    ppermute x2, waiting for transfers between devices: 18.2 us -> 25.3 us  [head_gather(): lax.ppermute(block, 'head', cross_perm(count, step))]
  transfers between devices with their start and end apart: 12 -> 12, of which waited for: 9 -> 9; matrix products, arithmetic and copies ran while one was open for 21% -> 25% of each run, Pallas kernels for 0% -> 0%
where the time goes in v4:
time: 431 us; the launch traced here: 429 us
  waiting for transfers between devices  214 us (50%)
  matrix products  73.2 us (17%)
  local copies, waits for them, and re-layouts  42.9 us (10%)
  starting transfers between devices  36.8 us (9%)
  other arithmetic  30.7 us (7%)
  Pallas kernels  30.5 us (7%)
    all_to_all x2, waiting for transfers between devices, body(): lax.all_to_all(outgoing[:, c], ('head', 'tok'), split_axis=0, concat_axis...  103 us
    all_to_all x2, waiting for transfers between devices, body(): lax.all_to_all(expert_part, ('head', 'tok'), split_axis=0, concat_axis=0,...  67.5 us
    pallas_call x1, Pallas kernels, attention(): pl.pallas_call(attention_kernel, grid_spec=grid_spec, out_shape=jax.Shape...  30.5 us
    dot_general x2, matrix products, body(): jnp.einsum('gsd,dju->jgsu', received[c], w_pair, preferred_element_type=j...  29.6 us
    ppermute x2, waiting for transfers between devices, head_gather(): lax.ppermute(block, 'head', cross_perm(count, step))  25.3 us
    dot_general x2, matrix products, body(): jnp.einsum('gsu,ud->gsd', hidden_part, w_down[c], preferred_element_type=...  19.1 us
    slice x1, local copies, waits for them, and re-layouts, body(): w_pair = w_expert[:, :, c * unit_count:(c + 1) * unit_count]  18.9 us
    all_to_all x2, starting transfers between devices, body(): lax.all_to_all(expert_part, ('head', 'tok'), split_axis=0, concat_axis=0,...  18.4 us
  transfers between devices with their start and end apart: 12, of which 9 were waited for; matrix products, arithmetic and copies ran while one was open for 25% of the time, Pallas kernels for 0%

profile of v4, /device:TPU:0, one launch (start us, length us, event | category | flops | bytes accessed | tf_op | source)
XLA Modules:
  0.0 429.0 jit_solution(1267776165673146905)
XLA Ops:
  0.0 2.9 collective-permute-start
  8.5 6.7 %collective-permute-done = bf16[128,2048]{1,0:T(8,128)(2,1)} collective-permute-done((bf16[128,2048]{1,0:T(8,128)(2,1)}, bf16[128,2048]{1,0:T(8,128)(2,1)}, u32[]{:S(2)}, u32[]{:S(2)}) %collective-permute-start) | collective-permute-done | bytes 524320 | tf_op jit(solution)/shard_map/ppermute | solution.py:146
  30.4 5.1 %fusion.29.q_ref.kn_ref.vn_ref = f32[512,1536]{1,0:T(8,128)} fusion(bf16[2048,1536]{1,0:T(8,128)(2,1)S(1)} %bitcast.210, bf16[1,512,2048]{2,1,0:T(8,128)(2,1)S(1)} %bitcast.199, f32[2048]{0:T(1024)S(1)} %copy-done.11, f32[512]{0:T(512)S(1)} %add_rsqrt_fusion), kind=kOutput, calls=%fused_computation.40 | convolution fusion | flops 3225419776 | bytes 11544576 | tf_op jit(solution)/shard_map/dot_general | solution.py:216
  35.5 30.5 %cached_attention.1 = bf16[512,512]{1,0:T(8,128)(2,1)} custom-call(s32[1]{0:T(128)} %copy.98.len_ref, f32[512,1536]{1,0:T(8,128)} %fusion.29.q_ref.kn_ref.vn_ref, f32[512,1536]{1,0:T(8,128)} %fusion.29.q_ref.kn_ref.vn_ref, f32[512,1536]{1,0:T(8,128)} %fusion.29.q_ref.kn_ref.vn_ref, f32[512,128]{1,0:T(8,128)} %get-tuple-element.47.cq_ref.ck_ref, ...), custom_call_target="tpu_custom_call" | custom-call | tf_op jit(solution)/shard_map/cached_attention/pallas_call | solution.py:127
  66.0 3.0 convolution_convert_fusion.2
  81.0 12.8 %collective-permute-done.3 = bf16[128,2048]{1,0:T(8,128)(2,1)} collective-permute-done((bf16[128,2048]{1,0:T(8,128)(2,1)}, bf16[128,2048]{1,0:T(8,128)(2,1)}, u32[]{:S(2)}, u32[]{:S(2)}) %collective-permute-start.3) | collective-permute-done | bytes 524320 | tf_op jit(solution)/shard_map/ppermute | solution.py:170
  99.3 3.2 slice_bitcast_fusion.1
  102.5 6.2 %all-to-all-start.1 = ((bf16[32,24,2048]{2,1,0:T(8,128)(2,1)}), bf16[32,24,2048]{2,1,0:T(8,128)(2,1)}, u32[]{:S(2)}, u32[]{:S(2)}) async-start(bf16[32,24,2048]{2,1,0:T(8,128)(2,1)} %get-tuple-element.37), calls=%async_computation.1 | async-start | bytes 6291456 | tf_op jit(solution)/shard_map/all_to_all | solution.py:247
  108.7 18.9 %fusion.54 = (bf16[2048,2,1408]{2,1,0:T(2,128)(2,1)}, bf16[2048,2,1408]{2,1,0:T(2,128)(2,1)}) fusion(bf16[2048,2,2816]{2,1,0:T(2,128)(2,1)} %param.32), kind=kLoop, calls=%fused_computation.113 | loop fusion | bytes 46137344 | tf_op jit(solution)/shard_map/slice | solution.py:253
  127.6 54.2 %all-to-all-done.1 = bf16[32,24,2048]{2,1,0:T(8,128)(2,1)} async-done(((bf16[32,24,2048]{2,1,0:T(8,128)(2,1)}), bf16[32,24,2048]{2,1,0:T(8,128)(2,1)}, u32[]{:S(2)}, u32[]{:S(2)}) %all-to-all-start.1) | async-done | bytes 3145760 | tf_op jit(solution)/shard_map/all_to_all | solution.py:247
  181.8 3.5 all-to-all-start
  185.3 14.8 %fusion.9 = f32[2,32,24,1408]{3,2,0,1:T(8,128)S(1)} fusion(bf16[2048,2,1408]{2,1,0:T(2,128)(2,1)} %get-tuple-element.35, bf16[32,24,2048]{2,1,0:T(8,128)(2,1)} %all-to-all-done.1), kind=kOutput, calls=%fused_computation.14 | convolution fusion | flops 8858370048 | bytes 23330816 | tf_op jit(solution)/shard_map/gsd,dju->jgsu/dot_general | solution.py:254
  200.1 9.5 %fusion.18 = bf16[32,24,2048]{2,1,0:T(8,128)(2,1)} fusion(bf16[2816,2048]{1,0:T(8,128)(2,1)} %param.33, f32[2,32,24,1408]{3,2,0,1:T(8,128)S(1)} %fusion.9), kind=kOutput, calls=%fused_computation.28 | convolution fusion | flops 4437245952 | bytes 17563648 | tf_op jit(solution)/shard_map/gsu,ud->gsd/dot_general | solution.py:258
  209.7 48.7 %all-to-all-done = bf16[32,24,2048]{2,1,0:T(8,128)(2,1)} async-done(((bf16[32,24,2048]{2,1,0:T(8,128)(2,1)}), bf16[32,24,2048]{2,1,0:T(8,128)(2,1)}, u32[]{:S(2)}, u32[]{:S(2)}) %all-to-all-start) | async-done | bytes 3145760 | tf_op jit(solution)/shard_map/all_to_all | solution.py:247
  258.4 14.9 %all-to-all-start.2 = ((bf16[32,24,2048]{2,1,0:T(8,128)(2,1)}), bf16[32,24,2048]{2,1,0:T(8,128)(2,1)}, u32[]{:S(2)}, u32[]{:S(2)}) async-start(bf16[32,24,2048]{2,1,0:T(8,128)(2,1)} %fusion.18), calls=%async_computation.2 | async-start | bytes 6291456 | tf_op jit(solution)/shard_map/all_to_all | solution.py:263
  273.3 14.8 %fusion.8 = f32[2,32,24,1408]{3,2,0,1:T(8,128)S(1)} fusion(bf16[2048,2,1408]{2,1,0:T(2,128)(2,1)} %get-tuple-element.34, bf16[32,24,2048]{2,1,0:T(8,128)(2,1)} %all-to-all-done), kind=kOutput, calls=%fused_computation.13 | convolution fusion | flops 8858370048 | bytes 23330816 | tf_op jit(solution)/shard_map/gsd,dju->jgsu/dot_general | solution.py:254
  288.1 9.5 %fusion.15 = bf16[32,24,2048]{2,1,0:T(8,128)(2,1)} fusion(bf16[2816,2048]{1,0:T(8,128)(2,1)} %param.33, f32[2,32,24,1408]{3,2,0,1:T(8,128)S(1)} %fusion.8), kind=kOutput, calls=%fused_computation.27 | convolution fusion | flops 4437245952 | bytes 17563648 | tf_op jit(solution)/shard_map/gsu,ud->gsd/dot_general | solution.py:258
  299.2 18.5 %collective-permute-done.4 = bf16[128,2048]{1,0:T(8,128)(2,1)S(1)} collective-permute-done((bf16[128,2048]{1,0:T(8,128)(2,1)S(1)}, bf16[128,2048]{1,0:T(8,128)(2,1)S(1)}, u32[]{:S(2)}, u32[]{:S(2)}) %collective-permute-start.4) | collective-permute-done | bytes 524320 | tf_op jit(solution)/shard_map/ppermute | solution.py:146
  321.6 24.5 %all-to-all-done.2 = bf16[32,24,2048]{2,1,0:T(8,128)(2,1)} async-done(((bf16[32,24,2048]{2,1,0:T(8,128)(2,1)}), bf16[32,24,2048]{2,1,0:T(8,128)(2,1)}, u32[]{:S(2)}, u32[]{:S(2)}) %all-to-all-start.2) | async-done | bytes 3145760 | tf_op jit(solution)/shard_map/all_to_all | solution.py:263
  346.1 3.5 all-to-all-start.3
  356.9 3.2 convolution_bitcast_fusion
  375.1 4.5 %fusion.57 = f32[128,2048]{1,0:T(8,128)} fusion(f32[128,768]{0,1:T(8,128)S(1)} %bitcast.204, bf16[768,2048]{1,0:T(8,128)(2,1)} %bitcast.49), kind=kOutput, calls=%fused_computation.116 | convolution fusion | flops 2415919104 | bytes 4587520 | tf_op jit(solution)/shard_map/dot_general | solution.py:265
  379.6 43.1 %all-to-all-done.3 = bf16[32,24,2048]{2,1,0:T(8,128)(2,1)} async-done(((bf16[32,24,2048]{2,1,0:T(8,128)(2,1)}), bf16[32,24,2048]{2,1,0:T(8,128)(2,1)}, u32[]{:S(2)}, u32[]{:S(2)}) %all-to-all-start.3) | async-done | bytes 3145760 | tf_op jit(solution)/shard_map/all_to_all | solution.py:263
  422.7 4.0 fusion.23
  (98 shorter events, 67.2 us)
Async XLA Ops:
  0.0 360.1 %copy-start = (bf16[704,2048]{1,0:T(8,128)(2,1)S(1)}, bf16[704,2048]{1,0:T(8,128)(2,1)}, u32[]{:S(2)}) copy-start(bf16[704,2048]{1,0:T(8,128)(2,1)} %param.28) | copy-start | bytes 8650756
  0.0 15.2 %collective-permute-start = (bf16[128,2048]{1,0:T(8,128)(2,1)}, bf16[128,2048]{1,0:T(8,128)(2,1)}, u32[]{:S(2)}, u32[]{:S(2)}) collective-permute-start(bf16[128,2048]{1,0:T(8,128)(2,1)} %bitcast.203), channel_id=1, source_target_pairs={{0,16},{8,24},{16,0},{24,8},{1,17},{9,25},{17,1},{25,9},{2,18},{10... | collective-permute-start | bytes 1572872 | tf_op jit(solution)/shard_map/ppermute | solution.py:146
  22.6 4.3 %collective-permute-start.1 = (bf16[2,128,2048]{2,1,0:T(8,128)(2,1)}, bf16[2,128,2048]{2,1,0:T(8,128)(2,1)}, u32[]{:S(2)}, u32[]{:S(2)}) collective-permute-start(bf16[2,128,2048]{2,1,0:T(8,128)(2,1)} %broadcast_select_fusion.1), channel_id=1, source_target_pairs={{0,8},{8,0},{16,24},{24,16},{1,9},{9,1},{17,25},{25,17},{2,10},{10... | collective-permute-start | bytes 3145736 | tf_op jit(solution)/shard_map/ppermute | solution.py:151
  22.8 4.1 copy-start.1
  27.0 2.6 slice-start
  28.5 1.8 slice-start.1
  28.8 1.6 copy-start.11
  71.5 3.2 collective-permute-start.2
  72.0 21.8 %copy-start.9 = (bf16[1,128,2048]{2,1,0:T(8,128)(2,1)S(1)}, bf16[1,128,2048]{2,1,0:T(8,128)(2,1)}, u32[]{:S(2)}) copy-start(bf16[1,128,2048]{2,1,0:T(8,128)(2,1)} %param.19) | copy-start | bytes 1572868
  78.4 17.9 %copy-start.10 = (f32[2048]{0:T(1024)S(1)}, f32[2048]{0:T(1024)}, u32[]{:S(2)}) copy-start(f32[2048]{0:T(1024)} %param.26) | copy-start | bytes 24580
  79.3 14.5 %collective-permute-start.3 = (bf16[128,2048]{1,0:T(8,128)(2,1)}, bf16[128,2048]{1,0:T(8,128)(2,1)}, u32[]{:S(2)}, u32[]{:S(2)}) collective-permute-start(bf16[128,2048]{1,0:T(8,128)(2,1)} %bitcast_convert_fusion.1), channel_id=1, source_target_pairs={{0,16},{8,24},{16,0},{24,8},{1,17},{9,25},{17,1},{25,9},{2,18},{10... | collective-permute-start | bytes 1572872 | tf_op jit(solution)/shard_map/ppermute | solution.py:170
  102.5 79.2 %all-to-all-start.1 = ((bf16[32,24,2048]{2,1,0:T(8,128)(2,1)}), bf16[32,24,2048]{2,1,0:T(8,128)(2,1)}, u32[]{:S(2)}, u32[]{:S(2)}) async-start(bf16[32,24,2048]{2,1,0:T(8,128)(2,1)} %get-tuple-element.37), calls=%async_computation.1 | async-start | bytes 6291456 | tf_op jit(solution)/shard_map/all_to_all | solution.py:247
  181.8 76.6 %all-to-all-start = ((bf16[32,24,2048]{2,1,0:T(8,128)(2,1)}), bf16[32,24,2048]{2,1,0:T(8,128)(2,1)}, u32[]{:S(2)}, u32[]{:S(2)}) async-start(bf16[32,24,2048]{2,1,0:T(8,128)(2,1)} %get-tuple-element.36), calls=%async_computation | async-start | bytes 6291456 | tf_op jit(solution)/shard_map/all_to_all | solution.py:247
  258.4 87.6 %all-to-all-start.2 = ((bf16[32,24,2048]{2,1,0:T(8,128)(2,1)}), bf16[32,24,2048]{2,1,0:T(8,128)(2,1)}, u32[]{:S(2)}, u32[]{:S(2)}) async-start(bf16[32,24,2048]{2,1,0:T(8,128)(2,1)} %fusion.18), calls=%async_computation.2 | async-start | bytes 6291456 | tf_op jit(solution)/shard_map/all_to_all | solution.py:263
  297.6 20.1 %collective-permute-start.4 = (bf16[128,2048]{1,0:T(8,128)(2,1)S(1)}, bf16[128,2048]{1,0:T(8,128)(2,1)S(1)}, u32[]{:S(2)}, u32[]{:S(2)}) collective-permute-start(bf16[128,2048]{1,0:T(8,128)(2,1)S(1)} %bitcast.200), channel_id=1, source_target_pairs={{0,16},{8,24},{16,0},{24,8},{1,17},{9,25},{17,1},{25,9},{2,18},{10... | collective-permute-start | bytes 1572872 | tf_op jit(solution)/shard_map/ppermute | solution.py:146
  346.1 76.6 %all-to-all-start.3 = ((bf16[32,24,2048]{2,1,0:T(8,128)(2,1)}), bf16[32,24,2048]{2,1,0:T(8,128)(2,1)}, u32[]{:S(2)}, u32[]{:S(2)}) async-start(bf16[32,24,2048]{2,1,0:T(8,128)(2,1)} %fusion.15), calls=%async_computation.3 | async-start | bytes 6291456 | tf_op jit(solution)/shard_map/all_to_all | solution.py:263
  351.0 2.7 collective-permute-start.5
  353.7 2.5 slice-start.2
  355.3 1.6 slice-start.3
  362.1 1.4 copy-start.3
  364.5 4.3 %collective-permute-start.6 = (bf16[2,128,2048]{2,1,0:T(8,128)(2,1)}, bf16[2,128,2048]{2,1,0:T(8,128)(2,1)}, u32[]{:S(2)}, u32[]{:S(2)}) collective-permute-start(bf16[2,128,2048]{2,1,0:T(8,128)(2,1)} %select_bitcast_fusion), channel_id=1, source_target_pairs={{0,8},{8,0},{16,24},{24,16},{1,9},{9,1},{17,25},{25,17},{2,10},{10... | collective-permute-start | bytes 3145736 | tf_op jit(solution)/shard_map/ppermute | solution.py:165
  373.5 53.2 %collective-permute-start.7 = (bf16[128,2048]{1,0:T(8,128)(2,1)}, bf16[128,2048]{1,0:T(8,128)(2,1)}, u32[]{:S(2)}, u32[]{:S(2)}) collective-permute-start(bf16[128,2048]{1,0:T(8,128)(2,1)} %bitcast_convert_fusion), channel_id=1, source_target_pairs={{0,16},{8,24},{16,0},{24,8},{1,17},{9,25},{17,1},{25,9},{2,18},{10... | collective-permute-start | bytes 1572872 | tf_op jit(solution)/shard_map/ppermute | solution.py:170
  379.6 47.1 %copy-start.8 = (bf16[1,128,2048]{2,1,0:T(8,128)(2,1)S(1)}, bf16[1,128,2048]{2,1,0:T(8,128)(2,1)}, u32[]{:S(2)}) copy-start(bf16[1,128,2048]{2,1,0:T(8,128)(2,1)} %copy-done.7) | copy-start | bytes 1572868
  422.7 4.0 copy-start.6
  (4 other events, 4.8 us)

commit v5 on v4

--- a/solution.py
+++ b/solution.py
@@ -72,42 +72,57 @@
     cache_rows = ko_ref.shape[1]
     length = len_ref[0]
     start = pl.program_id(1) * rows
-    factor = 1.0 / math.sqrt(q_ref.shape[-1])
-    contract = (((1,), (1,)), ((), ()))
-    queries = rotate(q_ref[...], cq_ref[...], sq_ref[...]).astype(jnp.bfloat16)
-    keys_new = rotate(kn_ref[...], ck_ref[...], sk_ref[...]).astype(jnp.bfloat16)
-    values_new = vn_ref[...].astype(jnp.bfloat16)
-    score_old = (
-        lax.dot_general(queries, ko_ref[0], contract, preferred_element_type=jnp.float32) * factor
-    )
-    score_new = (
-        lax.dot_general(queries, keys_new, contract, preferred_element_type=jnp.float32) * factor
-    )
-    live_old = lax.broadcasted_iota(jnp.int32, (rows, cache_rows), 1) < length
-    new_cols = lax.broadcasted_iota(jnp.int32, (rows, new_len), 1)
-    new_rows = lax.broadcasted_iota(jnp.int32, (rows, new_len), 0) + start
-    live_new = new_cols <= new_rows
-    row_max = jnp.maximum(
-        jnp.max(jnp.where(live_old, score_old, NEG_BIG), axis=1, keepdims=True),
-        jnp.max(jnp.where(live_new, score_new, NEG_BIG), axis=1, keepdims=True),
-    )
-    prob_old = jnp.where(live_old, jnp.exp(score_old - row_max), 0.0)
-    prob_new = jnp.where(live_new, jnp.exp(score_new - row_max), 0.0)
-    denom = jnp.sum(prob_old, axis=1, keepdims=True) + jnp.sum(prob_new, axis=1, keepdims=True)
-    weighted = jnp.dot(
-        prob_old.astype(jnp.bfloat16), vo_ref[0], preferred_element_type=jnp.float32
-    )
-    weighted = weighted + jnp.dot(
-        prob_new.astype(jnp.bfloat16), values_new, preferred_element_type=jnp.float32
-    )
-    o_ref[...] = (weighted / denom).astype(o_ref.dtype)
+
+    def compute(mask_cache):
+        factor = 1.0 / math.sqrt(q_ref.shape[-1])
+        contract = (((1,), (1,)), ((), ()))
+        queries = rotate(q_ref[...], cq_ref[...], sq_ref[...]).astype(jnp.bfloat16)
+        keys_new = rotate(kn_ref[...], ck_ref[...], sk_ref[...]).astype(jnp.bfloat16)
+        values_new = vn_ref[...].astype(jnp.bfloat16)
+        score_old = (
+            lax.dot_general(queries, ko_ref[0], contract, preferred_element_type=jnp.float32)
+            * factor
+        )
+        score_new = (
+            lax.dot_general(queries, keys_new, contract, preferred_element_type=jnp.float32)
+            * factor
+        )
+        if mask_cache:
+            live_old = lax.broadcasted_iota(jnp.int32, (rows, cache_rows), 1) < length
+            score_old = jnp.where(live_old, score_old, NEG_BIG)
+        new_cols = lax.broadcasted_iota(jnp.int32, (rows, new_len), 1)
+        new_rows = lax.broadcasted_iota(jnp.int32, (rows, new_len), 0) + start
+        score_new = jnp.where(new_cols <= new_rows, score_new, NEG_BIG)
+        row_max = jnp.maximum(
+            jnp.max(score_old, axis=1, keepdims=True), jnp.max(score_new, axis=1, keepdims=True)
+        )
+        prob_old = jnp.exp(score_old - row_max)
+        prob_new = jnp.exp(score_new - row_max)
+        denom = jnp.sum(prob_old, axis=1, keepdims=True) + jnp.sum(
+            prob_new, axis=1, keepdims=True
+        )
+        weighted = jnp.dot(
+            prob_old.astype(jnp.bfloat16), vo_ref[0], preferred_element_type=jnp.float32
+        )
+        weighted = weighted + jnp.dot(
+            prob_new.astype(jnp.bfloat16), values_new, preferred_element_type=jnp.float32
+        )
+        o_ref[...] = (weighted / denom).astype(o_ref.dtype)
+
+    @pl.when(length >= cache_rows)
+    def _():
+        compute(False)
+
+    @pl.when(length < cache_rows)
+    def _():
+        compute(True)
 
 
 def attention(length, qkv, cosine, sine_signed, k_cache, v_cache):
     new_len = qkv.shape[0]
     cache_rows = k_cache.shape[1]
     heads = qkv.shape[1] // (3 * HD)
-    rows = min(128, new_len)
+    rows = min(256, new_len)
     grid_spec = pltpu.PrefetchScalarGridSpec(
         num_scalar_prefetch=1,
         grid=(heads, new_len // rows),

time: 431 us -> 426 us (0.988)
  Pallas kernels: 30.5 us -> 24.3 us
    pallas_call x1, Pallas kernels: 30.5 us -> 24.3 us  [attention(): pl.pallas_call(attention_kernel, grid_spec=grid_spec, out_shape=jax.Shape...]
where the time goes in v5:
time: 426 us; the launch traced here: 422 us
  waiting for transfers between devices  214 us (50%)
  matrix products  73.2 us (17%)
  local copies, waits for them, and re-layouts  42.9 us (10%)
  starting transfers between devices  36.2 us (8%)
  other arithmetic  30.7 us (7%)
  Pallas kernels  24.3 us (6%)
    all_to_all x2, waiting for transfers between devices, body(): lax.all_to_all(outgoing[:, c], ('head', 'tok'), split_axis=0, concat_axis...  103 us
    all_to_all x2, waiting for transfers between devices, body(): lax.all_to_all(expert_part, ('head', 'tok'), split_axis=0, concat_axis=0,...  67.5 us
    dot_general x2, matrix products, body(): jnp.einsum('gsd,dju->jgsu', received[c], w_pair, preferred_element_type=j...  29.6 us
    ppermute x2, waiting for transfers between devices, head_gather(): lax.ppermute(block, 'head', cross_perm(count, step))  25.3 us
    pallas_call x1, Pallas kernels, attention(): pl.pallas_call(attention_kernel, grid_spec=grid_spec, out_shape=jax.Shape...  24.3 us
    dot_general x2, matrix products, body(): jnp.einsum('gsu,ud->gsd', hidden_part, w_down[c], preferred_element_type=...  19.1 us
    slice x1, local copies, waits for them, and re-layouts, body(): w_pair = w_expert[:, :, c * unit_count:(c + 1) * unit_count]  18.9 us
    all_to_all x2, starting transfers between devices, body(): lax.all_to_all(expert_part, ('head', 'tok'), split_axis=0, concat_axis=0,...  18.4 us
  transfers between devices with their start and end apart: 12, of which 9 were waited for; matrix products, arithmetic and copies ran while one was open for 25% of the time, Pallas kernels for 0%

profile of v5, /device:TPU:0, one launch (start us, length us, event | category | flops | bytes accessed | tf_op | source)
XLA Modules:
  0.0 422.2 jit_solution(18123963353068072483)
XLA Ops:
  0.0 2.9 collective-permute-start
  8.5 6.7 %collective-permute-done = bf16[128,2048]{1,0:T(8,128)(2,1)} collective-permute-done((bf16[128,2048]{1,0:T(8,128)(2,1)}, bf16[128,2048]{1,0:T(8,128)(2,1)}, u32[]{:S(2)}, u32[]{:S(2)}) %collective-permute-start) | collective-permute-done | bytes 524320 | tf_op jit(solution)/shard_map/ppermute | solution.py:161
  30.4 5.1 %fusion.29.q_ref.kn_ref.vn_ref = f32[512,1536]{1,0:T(8,128)} fusion(bf16[2048,1536]{1,0:T(8,128)(2,1)S(1)} %bitcast.210, bf16[1,512,2048]{2,1,0:T(8,128)(2,1)S(1)} %bitcast.199, f32[2048]{0:T(1024)S(1)} %copy-done.11, f32[512]{0:T(512)S(1)} %add_rsqrt_fusion), kind=kOutput, calls=%fused_computation.40 | convolution fusion | flops 3225419776 | bytes 11544576 | tf_op jit(solution)/shard_map/dot_general | solution.py:231
  35.5 24.3 %cached_attention.1 = bf16[512,512]{1,0:T(8,128)(2,1)} custom-call(s32[1]{0:T(128)} %copy.98.len_ref, f32[512,1536]{1,0:T(8,128)} %fusion.29.q_ref.kn_ref.vn_ref, f32[512,1536]{1,0:T(8,128)} %fusion.29.q_ref.kn_ref.vn_ref, f32[512,1536]{1,0:T(8,128)} %fusion.29.q_ref.kn_ref.vn_ref, f32[512,128]{1,0:T(8,128)} %get-tuple-element.47.cq_ref.ck_ref, ...), custom_call_target="tpu_custom_call" | custom-call | tf_op jit(solution)/shard_map/cached_attention/pallas_call | solution.py:142
  59.8 3.0 convolution_convert_fusion.2
  74.7 12.8 %collective-permute-done.3 = bf16[128,2048]{1,0:T(8,128)(2,1)} collective-permute-done((bf16[128,2048]{1,0:T(8,128)(2,1)}, bf16[128,2048]{1,0:T(8,128)(2,1)}, u32[]{:S(2)}, u32[]{:S(2)}) %collective-permute-start.3) | collective-permute-done | bytes 524320 | tf_op jit(solution)/shard_map/ppermute | solution.py:185
  93.1 3.2 slice_bitcast_fusion.1
  96.3 5.7 %all-to-all-start.1 = ((bf16[32,24,2048]{2,1,0:T(8,128)(2,1)}), bf16[32,24,2048]{2,1,0:T(8,128)(2,1)}, u32[]{:S(2)}, u32[]{:S(2)}) async-start(bf16[32,24,2048]{2,1,0:T(8,128)(2,1)} %get-tuple-element.37), calls=%async_computation.1 | async-start | bytes 6291456 | tf_op jit(solution)/shard_map/all_to_all | solution.py:262
  101.9 18.9 %fusion.54 = (bf16[2048,2,1408]{2,1,0:T(2,128)(2,1)}, bf16[2048,2,1408]{2,1,0:T(2,128)(2,1)}) fusion(bf16[2048,2,2816]{2,1,0:T(2,128)(2,1)} %param.32), kind=kLoop, calls=%fused_computation.113 | loop fusion | bytes 46137344 | tf_op jit(solution)/shard_map/slice | solution.py:268
  120.8 54.2 %all-to-all-done.1 = bf16[32,24,2048]{2,1,0:T(8,128)(2,1)} async-done(((bf16[32,24,2048]{2,1,0:T(8,128)(2,1)}), bf16[32,24,2048]{2,1,0:T(8,128)(2,1)}, u32[]{:S(2)}, u32[]{:S(2)}) %all-to-all-start.1) | async-done | bytes 3145760 | tf_op jit(solution)/shard_map/all_to_all | solution.py:262
  175.0 3.5 all-to-all-start
  178.6 14.8 %fusion.9 = f32[2,32,24,1408]{3,2,0,1:T(8,128)S(1)} fusion(bf16[2048,2,1408]{2,1,0:T(2,128)(2,1)} %get-tuple-element.35, bf16[32,24,2048]{2,1,0:T(8,128)(2,1)} %all-to-all-done.1), kind=kOutput, calls=%fused_computation.14 | convolution fusion | flops 8858370048 | bytes 23330816 | tf_op jit(solution)/shard_map/gsd,dju->jgsu/dot_general | solution.py:269
  193.4 9.5 %fusion.18 = bf16[32,24,2048]{2,1,0:T(8,128)(2,1)} fusion(bf16[2816,2048]{1,0:T(8,128)(2,1)} %param.33, f32[2,32,24,1408]{3,2,0,1:T(8,128)S(1)} %fusion.9), kind=kOutput, calls=%fused_computation.28 | convolution fusion | flops 4437245952 | bytes 17563648 | tf_op jit(solution)/shard_map/gsu,ud->gsd/dot_general | solution.py:273
  202.9 48.7 %all-to-all-done = bf16[32,24,2048]{2,1,0:T(8,128)(2,1)} async-done(((bf16[32,24,2048]{2,1,0:T(8,128)(2,1)}), bf16[32,24,2048]{2,1,0:T(8,128)(2,1)}, u32[]{:S(2)}, u32[]{:S(2)}) %all-to-all-start) | async-done | bytes 3145760 | tf_op jit(solution)/shard_map/all_to_all | solution.py:262
  251.6 14.9 %all-to-all-start.2 = ((bf16[32,24,2048]{2,1,0:T(8,128)(2,1)}), bf16[32,24,2048]{2,1,0:T(8,128)(2,1)}, u32[]{:S(2)}, u32[]{:S(2)}) async-start(bf16[32,24,2048]{2,1,0:T(8,128)(2,1)} %fusion.18), calls=%async_computation.2 | async-start | bytes 6291456 | tf_op jit(solution)/shard_map/all_to_all | solution.py:278
  266.5 14.8 %fusion.8 = f32[2,32,24,1408]{3,2,0,1:T(8,128)S(1)} fusion(bf16[2048,2,1408]{2,1,0:T(2,128)(2,1)} %get-tuple-element.34, bf16[32,24,2048]{2,1,0:T(8,128)(2,1)} %all-to-all-done), kind=kOutput, calls=%fused_computation.13 | convolution fusion | flops 8858370048 | bytes 23330816 | tf_op jit(solution)/shard_map/gsd,dju->jgsu/dot_general | solution.py:269
  281.3 9.5 %fusion.15 = bf16[32,24,2048]{2,1,0:T(8,128)(2,1)} fusion(bf16[2816,2048]{1,0:T(8,128)(2,1)} %param.33, f32[2,32,24,1408]{3,2,0,1:T(8,128)S(1)} %fusion.8), kind=kOutput, calls=%fused_computation.27 | convolution fusion | flops 4437245952 | bytes 17563648 | tf_op jit(solution)/shard_map/gsu,ud->gsd/dot_general | solution.py:273
  292.4 18.5 %collective-permute-done.4 = bf16[128,2048]{1,0:T(8,128)(2,1)S(1)} collective-permute-done((bf16[128,2048]{1,0:T(8,128)(2,1)S(1)}, bf16[128,2048]{1,0:T(8,128)(2,1)S(1)}, u32[]{:S(2)}, u32[]{:S(2)}) %collective-permute-start.4) | collective-permute-done | bytes 524320 | tf_op jit(solution)/shard_map/ppermute | solution.py:161
  314.8 24.5 %all-to-all-done.2 = bf16[32,24,2048]{2,1,0:T(8,128)(2,1)} async-done(((bf16[32,24,2048]{2,1,0:T(8,128)(2,1)}), bf16[32,24,2048]{2,1,0:T(8,128)(2,1)}, u32[]{:S(2)}, u32[]{:S(2)}) %all-to-all-start.2) | async-done | bytes 3145760 | tf_op jit(solution)/shard_map/all_to_all | solution.py:278
  339.3 3.5 all-to-all-start.3
  350.2 3.2 convolution_bitcast_fusion
  368.3 4.5 %fusion.57 = f32[128,2048]{1,0:T(8,128)} fusion(f32[128,768]{0,1:T(8,128)S(1)} %bitcast.204, bf16[768,2048]{1,0:T(8,128)(2,1)} %bitcast.49), kind=kOutput, calls=%fused_computation.116 | convolution fusion | flops 2415919104 | bytes 4587520 | tf_op jit(solution)/shard_map/dot_general | solution.py:280
  372.8 43.1 %all-to-all-done.3 = bf16[32,24,2048]{2,1,0:T(8,128)(2,1)} async-done(((bf16[32,24,2048]{2,1,0:T(8,128)(2,1)}), bf16[32,24,2048]{2,1,0:T(8,128)(2,1)}, u32[]{:S(2)}, u32[]{:S(2)}) %all-to-all-start.3) | async-done | bytes 3145760 | tf_op jit(solution)/shard_map/all_to_all | solution.py:278
  415.9 4.0 fusion.23
  (98 shorter events, 67.2 us)
Async XLA Ops:
  0.0 353.4 %copy-start = (bf16[704,2048]{1,0:T(8,128)(2,1)S(1)}, bf16[704,2048]{1,0:T(8,128)(2,1)}, u32[]{:S(2)}) copy-start(bf16[704,2048]{1,0:T(8,128)(2,1)} %param.28) | copy-start | bytes 8650756
  0.0 15.2 %collective-permute-start = (bf16[128,2048]{1,0:T(8,128)(2,1)}, bf16[128,2048]{1,0:T(8,128)(2,1)}, u32[]{:S(2)}, u32[]{:S(2)}) collective-permute-start(bf16[128,2048]{1,0:T(8,128)(2,1)} %bitcast.203), channel_id=1, source_target_pairs={{0,16},{8,24},{16,0},{24,8},{1,17},{9,25},{17,1},{25,9},{2,18},{10... | collective-permute-start | bytes 1572872 | tf_op jit(solution)/shard_map/ppermute | solution.py:161
  22.6 4.3 %collective-permute-start.1 = (bf16[2,128,2048]{2,1,0:T(8,128)(2,1)}, bf16[2,128,2048]{2,1,0:T(8,128)(2,1)}, u32[]{:S(2)}, u32[]{:S(2)}) collective-permute-start(bf16[2,128,2048]{2,1,0:T(8,128)(2,1)} %broadcast_select_fusion.1), channel_id=1, source_target_pairs={{0,8},{8,0},{16,24},{24,16},{1,9},{9,1},{17,25},{25,17},{2,10},{10... | collective-permute-start | bytes 3145736 | tf_op jit(solution)/shard_map/ppermute | solution.py:166
  22.8 4.1 copy-start.1
  27.0 2.6 slice-start
  28.5 1.8 slice-start.1
  28.8 1.6 copy-start.11
  65.2 3.1 collective-permute-start.2
  65.7 21.8 %copy-start.9 = (bf16[1,128,2048]{2,1,0:T(8,128)(2,1)S(1)}, bf16[1,128,2048]{2,1,0:T(8,128)(2,1)}, u32[]{:S(2)}) copy-start(bf16[1,128,2048]{2,1,0:T(8,128)(2,1)} %param.19) | copy-start | bytes 1572868
  72.1 17.9 %copy-start.10 = (f32[2048]{0:T(1024)S(1)}, f32[2048]{0:T(1024)}, u32[]{:S(2)}) copy-start(f32[2048]{0:T(1024)} %param.26) | copy-start | bytes 24580
  73.0 14.5 %collective-permute-start.3 = (bf16[128,2048]{1,0:T(8,128)(2,1)}, bf16[128,2048]{1,0:T(8,128)(2,1)}, u32[]{:S(2)}, u32[]{:S(2)}) collective-permute-start(bf16[128,2048]{1,0:T(8,128)(2,1)} %bitcast_convert_fusion.1), channel_id=1, source_target_pairs={{0,16},{8,24},{16,0},{24,8},{1,17},{9,25},{17,1},{25,9},{2,18},{10... | collective-permute-start | bytes 1572872 | tf_op jit(solution)/shard_map/ppermute | solution.py:185
  96.3 78.8 %all-to-all-start.1 = ((bf16[32,24,2048]{2,1,0:T(8,128)(2,1)}), bf16[32,24,2048]{2,1,0:T(8,128)(2,1)}, u32[]{:S(2)}, u32[]{:S(2)}) async-start(bf16[32,24,2048]{2,1,0:T(8,128)(2,1)} %get-tuple-element.37), calls=%async_computation.1 | async-start | bytes 6291456 | tf_op jit(solution)/shard_map/all_to_all | solution.py:262
  175.0 76.6 %all-to-all-start = ((bf16[32,24,2048]{2,1,0:T(8,128)(2,1)}), bf16[32,24,2048]{2,1,0:T(8,128)(2,1)}, u32[]{:S(2)}, u32[]{:S(2)}) async-start(bf16[32,24,2048]{2,1,0:T(8,128)(2,1)} %get-tuple-element.36), calls=%async_computation | async-start | bytes 6291456 | tf_op jit(solution)/shard_map/all_to_all | solution.py:262
  251.6 87.6 %all-to-all-start.2 = ((bf16[32,24,2048]{2,1,0:T(8,128)(2,1)}), bf16[32,24,2048]{2,1,0:T(8,128)(2,1)}, u32[]{:S(2)}, u32[]{:S(2)}) async-start(bf16[32,24,2048]{2,1,0:T(8,128)(2,1)} %fusion.18), calls=%async_computation.2 | async-start | bytes 6291456 | tf_op jit(solution)/shard_map/all_to_all | solution.py:278
  290.9 20.1 %collective-permute-start.4 = (bf16[128,2048]{1,0:T(8,128)(2,1)S(1)}, bf16[128,2048]{1,0:T(8,128)(2,1)S(1)}, u32[]{:S(2)}, u32[]{:S(2)}) collective-permute-start(bf16[128,2048]{1,0:T(8,128)(2,1)S(1)} %bitcast.200), channel_id=1, source_target_pairs={{0,16},{8,24},{16,0},{24,8},{1,17},{9,25},{17,1},{25,9},{2,18},{10... | collective-permute-start | bytes 1572872 | tf_op jit(solution)/shard_map/ppermute | solution.py:161
  339.3 76.6 %all-to-all-start.3 = ((bf16[32,24,2048]{2,1,0:T(8,128)(2,1)}), bf16[32,24,2048]{2,1,0:T(8,128)(2,1)}, u32[]{:S(2)}, u32[]{:S(2)}) async-start(bf16[32,24,2048]{2,1,0:T(8,128)(2,1)} %fusion.15), calls=%async_computation.3 | async-start | bytes 6291456 | tf_op jit(solution)/shard_map/all_to_all | solution.py:278
  344.2 2.7 collective-permute-start.5
  346.9 2.5 slice-start.2
  348.5 1.6 slice-start.3
  355.3 1.4 copy-start.3
  357.8 4.3 %collective-permute-start.6 = (bf16[2,128,2048]{2,1,0:T(8,128)(2,1)}, bf16[2,128,2048]{2,1,0:T(8,128)(2,1)}, u32[]{:S(2)}, u32[]{:S(2)}) collective-permute-start(bf16[2,128,2048]{2,1,0:T(8,128)(2,1)} %select_bitcast_fusion), channel_id=1, source_target_pairs={{0,8},{8,0},{16,24},{24,16},{1,9},{9,1},{17,25},{25,17},{2,10},{10... | collective-permute-start | bytes 3145736 | tf_op jit(solution)/shard_map/ppermute | solution.py:180
  366.7 53.2 %collective-permute-start.7 = (bf16[128,2048]{1,0:T(8,128)(2,1)}, bf16[128,2048]{1,0:T(8,128)(2,1)}, u32[]{:S(2)}, u32[]{:S(2)}) collective-permute-start(bf16[128,2048]{1,0:T(8,128)(2,1)} %bitcast_convert_fusion), channel_id=1, source_target_pairs={{0,16},{8,24},{16,0},{24,8},{1,17},{9,25},{17,1},{25,9},{2,18},{10... | collective-permute-start | bytes 1572872 | tf_op jit(solution)/shard_map/ppermute | solution.py:185
  372.8 47.1 %copy-start.8 = (bf16[1,128,2048]{2,1,0:T(8,128)(2,1)S(1)}, bf16[1,128,2048]{2,1,0:T(8,128)(2,1)}, u32[]{:S(2)}) copy-start(bf16[1,128,2048]{2,1,0:T(8,128)(2,1)} %copy-done.7) | copy-start | bytes 1572868
  415.9 4.0 copy-start.6
  (4 other events, 4.8 us)

commit v6 on v4

--- a/solution.py
+++ b/solution.py
@@ -14,6 +14,7 @@
 
 EPS = 1e-06
 NEG_BIG = -1e30
+CHUNK = 512
 
 
 def normalize(values, gain_vector):
@@ -65,11 +66,13 @@
 
 
 def attention_kernel(
-    len_ref, q_ref, kn_ref, vn_ref, cq_ref, sq_ref, ck_ref, sk_ref, ko_ref, vo_ref, o_ref
+    len_ref, q_ref, kn_ref, vn_ref, cq_ref, sq_ref, ck_ref, sk_ref, ko_ref, vo_ref, o_ref, s_ref
 ):
     rows = q_ref.shape[0]
     new_len = kn_ref.shape[0]
     cache_rows = ko_ref.shape[1]
+    chunk = CHUNK if cache_rows % CHUNK == 0 else cache_rows
+    chunk_count = cache_rows // chunk
     length = len_ref[0]
     start = pl.program_id(1) * rows
     factor = 1.0 / math.sqrt(q_ref.shape[-1])
@@ -77,29 +80,54 @@
     queries = rotate(q_ref[...], cq_ref[...], sq_ref[...]).astype(jnp.bfloat16)
     keys_new = rotate(kn_ref[...], ck_ref[...], sk_ref[...]).astype(jnp.bfloat16)
     values_new = vn_ref[...].astype(jnp.bfloat16)
-    score_old = (
-        lax.dot_general(queries, ko_ref[0], contract, preferred_element_type=jnp.float32) * factor
-    )
     score_new = (
         lax.dot_general(queries, keys_new, contract, preferred_element_type=jnp.float32) * factor
     )
-    live_old = lax.broadcasted_iota(jnp.int32, (rows, cache_rows), 1) < length
     new_cols = lax.broadcasted_iota(jnp.int32, (rows, new_len), 1)
     new_rows = lax.broadcasted_iota(jnp.int32, (rows, new_len), 0) + start
-    live_new = new_cols <= new_rows
-    row_max = jnp.maximum(
-        jnp.max(jnp.where(live_old, score_old, NEG_BIG), axis=1, keepdims=True),
-        jnp.max(jnp.where(live_new, score_new, NEG_BIG), axis=1, keepdims=True),
-    )
-    prob_old = jnp.where(live_old, jnp.exp(score_old - row_max), 0.0)
-    prob_new = jnp.where(live_new, jnp.exp(score_new - row_max), 0.0)
-    denom = jnp.sum(prob_old, axis=1, keepdims=True) + jnp.sum(prob_new, axis=1, keepdims=True)
+    score_new = jnp.where(new_cols <= new_rows, score_new, NEG_BIG)
+    full = jnp.minimum(length // chunk, chunk_count)
+    partial = jnp.logical_and(full < chunk_count, length % chunk > 0)
+    live = full + partial.astype(jnp.int32)
+
+    def old_scores(index):
+        offset = pl.multiple_of(index * chunk, chunk)
+        keys = ko_ref[0, pl.ds(offset, chunk), :]
+        return lax.dot_general(queries, keys, contract, preferred_element_type=jnp.float32) * factor
+
+    def first_pass(index, row_max):
+        scores = old_scores(index)
+        s_ref[index] = scores
+        return jnp.maximum(row_max, jnp.max(scores, axis=1, keepdims=True))
+
+    row_max = lax.fori_loop(0, full, first_pass, jnp.max(score_new, axis=1, keepdims=True))
+    s_ref[full] = jnp.full((rows, chunk), NEG_BIG, jnp.float32)
+
+    @pl.when(partial)
+    def _():
+        scores = old_scores(full)
+        cols = lax.broadcasted_iota(jnp.int32, (rows, chunk), 1) + full * chunk
+        s_ref[full] = jnp.where(cols < length, scores, NEG_BIG)
+
+    row_max = jnp.maximum(row_max, jnp.max(s_ref[full], axis=1, keepdims=True))
+    prob_new = jnp.exp(score_new - row_max)
+    denom = jnp.sum(prob_new, axis=1, keepdims=True)
     weighted = jnp.dot(
-        prob_old.astype(jnp.bfloat16), vo_ref[0], preferred_element_type=jnp.float32
-    )
-    weighted = weighted + jnp.dot(
         prob_new.astype(jnp.bfloat16), values_new, preferred_element_type=jnp.float32
     )
+
+    def second_pass(index, carry):
+        denom, weighted = carry
+        probs = jnp.exp(s_ref[index] - row_max)
+        offset = pl.multiple_of(index * chunk, chunk)
+        values = vo_ref[0, pl.ds(offset, chunk), :]
+        denom = denom + jnp.sum(probs, axis=1, keepdims=True)
+        weighted = weighted + jnp.dot(
+            probs.astype(jnp.bfloat16), values, preferred_element_type=jnp.float32
+        )
+        return denom, weighted
+
+    denom, weighted = lax.fori_loop(0, live, second_pass, (denom, weighted))
     o_ref[...] = (weighted / denom).astype(o_ref.dtype)
 
 
@@ -107,7 +135,8 @@
     new_len = qkv.shape[0]
     cache_rows = k_cache.shape[1]
     heads = qkv.shape[1] // (3 * HD)
-    rows = min(128, new_len)
+    rows = min(256, new_len)
+    chunk = CHUNK if cache_rows % CHUNK == 0 else cache_rows
     grid_spec = pltpu.PrefetchScalarGridSpec(
         num_scalar_prefetch=1,
         grid=(heads, new_len // rows),
@@ -123,6 +152,7 @@
             pl.BlockSpec((1, cache_rows, HD), lambda h, i, n: (0, 0, h)),
         ],
         out_specs=pl.BlockSpec((rows, HD), lambda h, i, n: (i, h)),
+        scratch_shapes=[pltpu.VMEM((cache_rows // chunk + 1, rows, chunk), jnp.float32)],
     )
     return pl.pallas_call(
         attention_kernel,

time: 431 us -> 444 us (1.030)
  starting transfers between devices: 36.8 us -> 65.7 us
  Pallas kernels: 30.5 us -> 15.2 us
    all_to_all x2, starting transfers between devices: 9.71 us -> 38.7 us  [body(): lax.all_to_all(outgoing[:, c], ('head', 'tok'), split_axis=0, concat_axis...]
    pallas_call x1, Pallas kernels: 30.5 us -> 15.2 us  [attention(): pl.pallas_call(attention_kernel, grid_spec=grid_spec, out_shape=jax.Shape...]
  transfers between devices with their start and end apart: 12 -> 12, of which waited for: 9 -> 9; matrix products, arithmetic and copies ran while one was open for 25% -> 24% of each run, Pallas kernels for 0% -> 0%
where the time goes in v6:
time: 444 us; the launch traced here: 443 us
  waiting for transfers between devices  214 us (48%)
  matrix products  73.2 us (16%)
  starting transfers between devices  65.7 us (15%)
  local copies, waits for them, and re-layouts  42.9 us (10%)
  other arithmetic  30.7 us (7%)
  Pallas kernels  15.2 us (3%)
    all_to_all x2, waiting for transfers between devices, body(): lax.all_to_all(outgoing[:, c], ('head', 'tok'), split_axis=0, concat_axis...  103 us
    all_to_all x2, waiting for transfers between devices, body(): lax.all_to_all(expert_part, ('head', 'tok'), split_axis=0, concat_axis=0,...  67.5 us
    all_to_all x2, starting transfers between devices, body(): lax.all_to_all(outgoing[:, c], ('head', 'tok'), split_axis=0, concat_axis...  38.7 us
    dot_general x2, matrix products, body(): jnp.einsum('gsd,dju->jgsu', received[c], w_pair, preferred_element_type=j...  29.6 us
    ppermute x2, waiting for transfers between devices, head_gather(): lax.ppermute(block, 'head', cross_perm(count, step))  25.3 us
    dot_general x2, matrix products, body(): jnp.einsum('gsu,ud->gsd', hidden_part, w_down[c], preferred_element_type=...  19.1 us
    slice x1, local copies, waits for them, and re-layouts, body(): w_pair = w_expert[:, :, c * unit_count:(c + 1) * unit_count]  18.9 us
    all_to_all x2, starting transfers between devices, body(): lax.all_to_all(expert_part, ('head', 'tok'), split_axis=0, concat_axis=0,...  18.4 us
  transfers between devices with their start and end apart: 12, of which 9 were waited for; matrix products, arithmetic and copies ran while one was open for 24% of the time, Pallas kernels for 0%

profile of v6, /device:TPU:0, one launch (start us, length us, event | category | flops | bytes accessed | tf_op | source)
XLA Modules:
  0.0 442.6 jit_solution(10150710607960908809)
XLA Ops:
  0.0 2.9 collective-permute-start
  8.5 6.7 %collective-permute-done = bf16[128,2048]{1,0:T(8,128)(2,1)} collective-permute-done((bf16[128,2048]{1,0:T(8,128)(2,1)}, bf16[128,2048]{1,0:T(8,128)(2,1)}, u32[]{:S(2)}, u32[]{:S(2)}) %collective-permute-start) | collective-permute-done | bytes 524320 | tf_op jit(solution)/shard_map/ppermute | solution.py:176
  30.4 5.1 %fusion.29.q_ref.kn_ref.vn_ref = f32[512,1536]{1,0:T(8,128)} fusion(bf16[2048,1536]{1,0:T(8,128)(2,1)S(1)} %bitcast.210, bf16[1,512,2048]{2,1,0:T(8,128)(2,1)S(1)} %bitcast.199, f32[2048]{0:T(1024)S(1)} %copy-done.11, f32[512]{0:T(512)S(1)} %add_rsqrt_fusion), kind=kOutput, calls=%fused_computation.40 | convolution fusion | flops 3225419776 | bytes 11544576 | tf_op jit(solution)/shard_map/dot_general | solution.py:246
  35.5 15.2 %cached_attention.1 = bf16[512,512]{1,0:T(8,128)(2,1)} custom-call(s32[1]{0:T(128)} %copy.98.len_ref, f32[512,1536]{1,0:T(8,128)} %fusion.29.q_ref.kn_ref.vn_ref, f32[512,1536]{1,0:T(8,128)} %fusion.29.q_ref.kn_ref.vn_ref, f32[512,1536]{1,0:T(8,128)} %fusion.29.q_ref.kn_ref.vn_ref, f32[512,128]{1,0:T(8,128)} %get-tuple-element.47.cq_ref.ck_ref, ...), custom_call_target="tpu_custom_call" | custom-call | tf_op jit(solution)/shard_map/cached_attention/pallas_call | solution.py:157
  50.7 3.0 convolution_convert_fusion.2
  65.7 12.8 %collective-permute-done.3 = bf16[128,2048]{1,0:T(8,128)(2,1)} collective-permute-done((bf16[128,2048]{1,0:T(8,128)(2,1)}, bf16[128,2048]{1,0:T(8,128)(2,1)}, u32[]{:S(2)}, u32[]{:S(2)}) %collective-permute-start.3) | collective-permute-done | bytes 524320 | tf_op jit(solution)/shard_map/ppermute | solution.py:200
  84.0 3.2 slice_bitcast_fusion.1
  87.2 35.1 %all-to-all-start.1 = ((bf16[32,24,2048]{2,1,0:T(8,128)(2,1)}), bf16[32,24,2048]{2,1,0:T(8,128)(2,1)}, u32[]{:S(2)}, u32[]{:S(2)}) async-start(bf16[32,24,2048]{2,1,0:T(8,128)(2,1)} %get-tuple-element.37), calls=%async_computation.1 | async-start | bytes 6291456 | tf_op jit(solution)/shard_map/all_to_all | solution.py:277
  122.3 18.9 %fusion.54 = (bf16[2048,2,1408]{2,1,0:T(2,128)(2,1)}, bf16[2048,2,1408]{2,1,0:T(2,128)(2,1)}) fusion(bf16[2048,2,2816]{2,1,0:T(2,128)(2,1)} %param.32), kind=kLoop, calls=%fused_computation.113 | loop fusion | bytes 46137344 | tf_op jit(solution)/shard_map/slice | solution.py:283
  141.2 54.2 %all-to-all-done.1 = bf16[32,24,2048]{2,1,0:T(8,128)(2,1)} async-done(((bf16[32,24,2048]{2,1,0:T(8,128)(2,1)}), bf16[32,24,2048]{2,1,0:T(8,128)(2,1)}, u32[]{:S(2)}, u32[]{:S(2)}) %all-to-all-start.1) | async-done | bytes 3145760 | tf_op jit(solution)/shard_map/all_to_all | solution.py:277
  195.4 3.5 all-to-all-start
  198.9 14.8 %fusion.9 = f32[2,32,24,1408]{3,2,0,1:T(8,128)S(1)} fusion(bf16[2048,2,1408]{2,1,0:T(2,128)(2,1)} %get-tuple-element.35, bf16[32,24,2048]{2,1,0:T(8,128)(2,1)} %all-to-all-done.1), kind=kOutput, calls=%fused_computation.14 | convolution fusion | flops 8858370048 | bytes 23330816 | tf_op jit(solution)/shard_map/gsd,dju->jgsu/dot_general | solution.py:284
  213.7 9.5 %fusion.18 = bf16[32,24,2048]{2,1,0:T(8,128)(2,1)} fusion(bf16[2816,2048]{1,0:T(8,128)(2,1)} %param.33, f32[2,32,24,1408]{3,2,0,1:T(8,128)S(1)} %fusion.9), kind=kOutput, calls=%fused_computation.28 | convolution fusion | flops 4437245952 | bytes 17563648 | tf_op jit(solution)/shard_map/gsu,ud->gsd/dot_general | solution.py:288
  223.3 48.8 %all-to-all-done = bf16[32,24,2048]{2,1,0:T(8,128)(2,1)} async-done(((bf16[32,24,2048]{2,1,0:T(8,128)(2,1)}), bf16[32,24,2048]{2,1,0:T(8,128)(2,1)}, u32[]{:S(2)}, u32[]{:S(2)}) %all-to-all-start) | async-done | bytes 3145760 | tf_op jit(solution)/shard_map/all_to_all | solution.py:277
  272.0 14.9 %all-to-all-start.2 = ((bf16[32,24,2048]{2,1,0:T(8,128)(2,1)}), bf16[32,24,2048]{2,1,0:T(8,128)(2,1)}, u32[]{:S(2)}, u32[]{:S(2)}) async-start(bf16[32,24,2048]{2,1,0:T(8,128)(2,1)} %fusion.18), calls=%async_computation.2 | async-start | bytes 6291456 | tf_op jit(solution)/shard_map/all_to_all | solution.py:293
  286.9 14.8 %fusion.8 = f32[2,32,24,1408]{3,2,0,1:T(8,128)S(1)} fusion(bf16[2048,2,1408]{2,1,0:T(2,128)(2,1)} %get-tuple-element.34, bf16[32,24,2048]{2,1,0:T(8,128)(2,1)} %all-to-all-done), kind=kOutput, calls=%fused_computation.13 | convolution fusion | flops 8858370048 | bytes 23330816 | tf_op jit(solution)/shard_map/gsd,dju->jgsu/dot_general | solution.py:284
  301.7 9.5 %fusion.15 = bf16[32,24,2048]{2,1,0:T(8,128)(2,1)} fusion(bf16[2816,2048]{1,0:T(8,128)(2,1)} %param.33, f32[2,32,24,1408]{3,2,0,1:T(8,128)S(1)} %fusion.8), kind=kOutput, calls=%fused_computation.27 | convolution fusion | flops 4437245952 | bytes 17563648 | tf_op jit(solution)/shard_map/gsu,ud->gsd/dot_general | solution.py:288
  312.7 18.5 %collective-permute-done.4 = bf16[128,2048]{1,0:T(8,128)(2,1)S(1)} collective-permute-done((bf16[128,2048]{1,0:T(8,128)(2,1)S(1)}, bf16[128,2048]{1,0:T(8,128)(2,1)S(1)}, u32[]{:S(2)}, u32[]{:S(2)}) %collective-permute-start.4) | collective-permute-done | bytes 524320 | tf_op jit(solution)/shard_map/ppermute | solution.py:176
  335.2 24.5 %all-to-all-done.2 = bf16[32,24,2048]{2,1,0:T(8,128)(2,1)} async-done(((bf16[32,24,2048]{2,1,0:T(8,128)(2,1)}), bf16[32,24,2048]{2,1,0:T(8,128)(2,1)}, u32[]{:S(2)}, u32[]{:S(2)}) %all-to-all-start.2) | async-done | bytes 3145760 | tf_op jit(solution)/shard_map/all_to_all | solution.py:293
  359.6 3.5 all-to-all-start.3
  370.5 3.2 convolution_bitcast_fusion
  388.7 4.5 %fusion.57 = f32[128,2048]{1,0:T(8,128)} fusion(f32[128,768]{0,1:T(8,128)S(1)} %bitcast.204, bf16[768,2048]{1,0:T(8,128)(2,1)} %bitcast.49), kind=kOutput, calls=%fused_computation.116 | convolution fusion | flops 2415919104 | bytes 4587520 | tf_op jit(solution)/shard_map/dot_general | solution.py:295
  393.2 43.1 %all-to-all-done.3 = bf16[32,24,2048]{2,1,0:T(8,128)(2,1)} async-done(((bf16[32,24,2048]{2,1,0:T(8,128)(2,1)}), bf16[32,24,2048]{2,1,0:T(8,128)(2,1)}, u32[]{:S(2)}, u32[]{:S(2)}) %all-to-all-start.3) | async-done | bytes 3145760 | tf_op jit(solution)/shard_map/all_to_all | solution.py:293
  436.3 4.0 fusion.23
  (98 shorter events, 67.2 us)
Async XLA Ops:
  0.0 373.7 %copy-start = (bf16[704,2048]{1,0:T(8,128)(2,1)S(1)}, bf16[704,2048]{1,0:T(8,128)(2,1)}, u32[]{:S(2)}) copy-start(bf16[704,2048]{1,0:T(8,128)(2,1)} %param.28) | copy-start | bytes 8650756
  0.0 15.2 %collective-permute-start = (bf16[128,2048]{1,0:T(8,128)(2,1)}, bf16[128,2048]{1,0:T(8,128)(2,1)}, u32[]{:S(2)}, u32[]{:S(2)}) collective-permute-start(bf16[128,2048]{1,0:T(8,128)(2,1)} %bitcast.203), channel_id=1, source_target_pairs={{0,16},{8,24},{16,0},{24,8},{1,17},{9,25},{17,1},{25,9},{2,18},{10... | collective-permute-start | bytes 1572872 | tf_op jit(solution)/shard_map/ppermute | solution.py:176
  22.6 4.3 collective-permute-start.1
  22.8 4.1 copy-start.1
  27.0 2.6 slice-start
  28.5 1.8 slice-start.1
  28.8 1.6 copy-start.11
  56.2 3.1 collective-permute-start.2
  56.7 21.8 %copy-start.9 = (bf16[1,128,2048]{2,1,0:T(8,128)(2,1)S(1)}, bf16[1,128,2048]{2,1,0:T(8,128)(2,1)}, u32[]{:S(2)}) copy-start(bf16[1,128,2048]{2,1,0:T(8,128)(2,1)} %param.19) | copy-start | bytes 1572868
  63.0 17.9 %copy-start.10 = (f32[2048]{0:T(1024)S(1)}, f32[2048]{0:T(1024)}, u32[]{:S(2)}) copy-start(f32[2048]{0:T(1024)} %param.26) | copy-start | bytes 24580
  63.9 14.5 %collective-permute-start.3 = (bf16[128,2048]{1,0:T(8,128)(2,1)}, bf16[128,2048]{1,0:T(8,128)(2,1)}, u32[]{:S(2)}, u32[]{:S(2)}) collective-permute-start(bf16[128,2048]{1,0:T(8,128)(2,1)} %bitcast_convert_fusion.1), channel_id=1, source_target_pairs={{0,16},{8,24},{16,0},{24,8},{1,17},{9,25},{17,1},{25,9},{2,18},{10... | collective-permute-start | bytes 1572872 | tf_op jit(solution)/shard_map/ppermute | solution.py:200
  87.2 108.2 %all-to-all-start.1 = ((bf16[32,24,2048]{2,1,0:T(8,128)(2,1)}), bf16[32,24,2048]{2,1,0:T(8,128)(2,1)}, u32[]{:S(2)}, u32[]{:S(2)}) async-start(bf16[32,24,2048]{2,1,0:T(8,128)(2,1)} %get-tuple-element.37), calls=%async_computation.1 | async-start | bytes 6291456 | tf_op jit(solution)/shard_map/all_to_all | solution.py:277
  195.4 76.6 %all-to-all-start = ((bf16[32,24,2048]{2,1,0:T(8,128)(2,1)}), bf16[32,24,2048]{2,1,0:T(8,128)(2,1)}, u32[]{:S(2)}, u32[]{:S(2)}) async-start(bf16[32,24,2048]{2,1,0:T(8,128)(2,1)} %get-tuple-element.36), calls=%async_computation | async-start | bytes 6291456 | tf_op jit(solution)/shard_map/all_to_all | solution.py:277
  272.0 87.6 %all-to-all-start.2 = ((bf16[32,24,2048]{2,1,0:T(8,128)(2,1)}), bf16[32,24,2048]{2,1,0:T(8,128)(2,1)}, u32[]{:S(2)}, u32[]{:S(2)}) async-start(bf16[32,24,2048]{2,1,0:T(8,128)(2,1)} %fusion.18), calls=%async_computation.2 | async-start | bytes 6291456 | tf_op jit(solution)/shard_map/all_to_all | solution.py:293
  311.2 20.0 %collective-permute-start.4 = (bf16[128,2048]{1,0:T(8,128)(2,1)S(1)}, bf16[128,2048]{1,0:T(8,128)(2,1)S(1)}, u32[]{:S(2)}, u32[]{:S(2)}) collective-permute-start(bf16[128,2048]{1,0:T(8,128)(2,1)S(1)} %bitcast.200), channel_id=1, source_target_pairs={{0,16},{8,24},{16,0},{24,8},{1,17},{9,25},{17,1},{25,9},{2,18},{10... | collective-permute-start | bytes 1572872 | tf_op jit(solution)/shard_map/ppermute | solution.py:176
  359.6 76.6 %all-to-all-start.3 = ((bf16[32,24,2048]{2,1,0:T(8,128)(2,1)}), bf16[32,24,2048]{2,1,0:T(8,128)(2,1)}, u32[]{:S(2)}, u32[]{:S(2)}) async-start(bf16[32,24,2048]{2,1,0:T(8,128)(2,1)} %fusion.15), calls=%async_computation.3 | async-start | bytes 6291456 | tf_op jit(solution)/shard_map/all_to_all | solution.py:293
  364.6 2.7 collective-permute-start.5
  367.3 2.5 slice-start.2
  368.9 1.6 slice-start.3
  375.7 1.4 copy-start.3
  378.1 4.3 collective-permute-start.6
  387.1 53.2 %collective-permute-start.7 = (bf16[128,2048]{1,0:T(8,128)(2,1)}, bf16[128,2048]{1,0:T(8,128)(2,1)}, u32[]{:S(2)}, u32[]{:S(2)}) collective-permute-start(bf16[128,2048]{1,0:T(8,128)(2,1)} %bitcast_convert_fusion), channel_id=1, source_target_pairs={{0,16},{8,24},{16,0},{24,8},{1,17},{9,25},{17,1},{25,9},{2,18},{10... | collective-permute-start | bytes 1572872 | tf_op jit(solution)/shard_map/ppermute | solution.py:200
  393.2 47.1 %copy-start.8 = (bf16[1,128,2048]{2,1,0:T(8,128)(2,1)S(1)}, bf16[1,128,2048]{2,1,0:T(8,128)(2,1)}, u32[]{:S(2)}) copy-start(bf16[1,128,2048]{2,1,0:T(8,128)(2,1)} %copy-done.7) | copy-start | bytes 1572868
  436.3 4.0 copy-start.6
  (4 other events, 4.8 us)

commit v7 on v5

--- a/solution.py
+++ b/solution.py
@@ -223,11 +223,10 @@
     matches = (target[:, :, None] == columns[None, None, :]).astype(jnp.float32)
     placement = jnp.sum(matches, axis=1).astype(jnp.bfloat16)
     routing_matrix = jnp.sum(matches * expert_weights.reshape(local_rows, TOP)[:, :, None], axis=1)
-    gathered = head_gather(tokens[0])[None]
-    gathered, placement, routing_matrix = lax.optimization_barrier(
-        (gathered, placement, routing_matrix)
-    )
-    normed = normalize(gathered, attn_gain)
+    normed = head_gather(normalize(tokens[0], attn_gain))[None]
+    normed, placement, routing_matrix = lax.optimization_barrier(
+        (normed, placement, routing_matrix)
+    )
     qkv = jnp.dot(normed[0], w_qkv, preferred_element_type=jnp.float32)
     length = cache_len[0]
     positions = length + jnp.arange(new_len, dtype=jnp.int32)

time: 426 us -> 429 us (level)
  waiting for transfers between devices: 214 us -> 207 us
  other arithmetic: 30.7 us -> 37.2 us
    ppermute x2, waiting for transfers between devices: 25.3 us -> 18.8 us  [head_gather(): lax.ppermute(block, 'head', cross_perm(count, step))]
    unnamed x34 -> x40, local copies, waits for them, and re-layouts: 9.71 us -> 9.52 us
  transfers between devices with their start and end apart: 12 -> 12, of which waited for: 9 -> 9; matrix products, arithmetic and copies ran while one was open for 25% -> 26% of each run, Pallas kernels for 0% -> 0%
where the time goes in v7:
time: 429 us; the launch traced here: 425 us
  waiting for transfers between devices  207 us (48%)
  matrix products  72.1 us (17%)
  local copies, waits for them, and re-layouts  46 us (11%)
  other arithmetic  37.2 us (9%)
  starting transfers between devices  36.8 us (9%)
  Pallas kernels  24.2 us (6%)
    all_to_all x2, waiting for transfers between devices, body(): lax.all_to_all(outgoing[:, c], ('head', 'tok'), split_axis=0, concat_axis...  103 us
    all_to_all x2, waiting for transfers between devices, body(): lax.all_to_all(expert_part, ('head', 'tok'), split_axis=0, concat_axis=0,...  67.5 us
    dot_general x2, matrix products, body(): jnp.einsum('gsd,dju->jgsu', received[c], w_pair, preferred_element_type=j...  29.6 us
    pallas_call x1, Pallas kernels, attention(): pl.pallas_call(attention_kernel, grid_spec=grid_spec, out_shape=jax.Shape...  24.2 us
    dot_general x2, matrix products, body(): jnp.einsum('gsu,ud->gsd', hidden_part, w_down[c], preferred_element_type=...  19.1 us
    slice x1, local copies, waits for them, and re-layouts, body(): w_pair = w_expert[:, :, c * unit_count:(c + 1) * unit_count]  18.8 us
    ppermute x2, waiting for transfers between devices, head_gather(): lax.ppermute(block, 'head', cross_perm(count, step))  18.8 us
    all_to_all x2, starting transfers between devices, body(): lax.all_to_all(expert_part, ('head', 'tok'), split_axis=0, concat_axis=0,...  18.4 us
  transfers between devices with their start and end apart: 12, of which 9 were waited for; matrix products, arithmetic and copies ran while one was open for 26% of the time, Pallas kernels for 0%

profile of v7, /device:TPU:0, one launch (start us, length us, event | category | flops | bytes accessed | tf_op | source)
XLA Modules:
  0.0 425.0 jit_solution(672620115796371978)
XLA Ops:
  3.4 2.9 collective-permute-start
  8.0 4.4 %reduce-window.6 = s32[1,64,6,128]{3,1,2,0:T(8,128)} reduce-window(s32[1,64,6,128]{3,1,2,0:T(8,128)} %copy_bitcast_fusion.8, s32[]{:T(128)} %constant.101.clone.1), window={size=1x1x1x128 pad=0_0x0_0x0_0x127_0}, to_apply=%region_2.4 | reduce-window | flops 6242304 | bytes 393220 | tf_op jit(solution)/shard_map/reduce-window
  33.7 5.1 %fusion.25.q_ref.kn_ref.vn_ref = f32[512,1536]{1,0:T(8,128)} fusion(bf16[2048,1536]{1,0:T(8,128)(2,1)S(1)} %bitcast.217, bf16[1,512,2048]{2,1,0:T(8,128)(2,1)S(1)} %bitcast.209), kind=kOutput, calls=%fused_computation.38 | convolution fusion | flops 3221225472 | bytes 11534336 | tf_op jit(solution)/shard_map/dot_general | solution.py:230
  38.7 24.2 %cached_attention.1 = bf16[512,512]{1,0:T(8,128)(2,1)} custom-call(s32[1]{0:T(128)} %copy.98.len_ref, f32[512,1536]{1,0:T(8,128)} %fusion.25.q_ref.kn_ref.vn_ref, f32[512,1536]{1,0:T(8,128)} %fusion.25.q_ref.kn_ref.vn_ref, f32[512,1536]{1,0:T(8,128)} %fusion.25.q_ref.kn_ref.vn_ref, f32[512,128]{1,0:T(8,128)} %get-tuple-element.47.cq_ref.ck_ref, ...), custom_call_target="tpu_custom_call" | custom-call | tf_op jit(solution)/shard_map/cached_attention/pallas_call | solution.py:142
  63.0 3.0 convolution_convert_fusion.2
  77.9 12.8 %collective-permute-done.3 = bf16[128,2048]{1,0:T(8,128)(2,1)} collective-permute-done((bf16[128,2048]{1,0:T(8,128)(2,1)}, bf16[128,2048]{1,0:T(8,128)(2,1)}, u32[]{:S(2)}, u32[]{:S(2)}) %collective-permute-start.3) | collective-permute-done | bytes 524320 | tf_op jit(solution)/shard_map/ppermute | solution.py:185
  95.3 3.2 slice_bitcast_fusion.1
  98.4 6.2 %all-to-all-start.1 = ((bf16[32,24,2048]{2,1,0:T(8,128)(2,1)}), bf16[32,24,2048]{2,1,0:T(8,128)(2,1)}, u32[]{:S(2)}, u32[]{:S(2)}) async-start(bf16[32,24,2048]{2,1,0:T(8,128)(2,1)} %get-tuple-element.37), calls=%async_computation.1 | async-start | bytes 6291456 | tf_op jit(solution)/shard_map/all_to_all | solution.py:261
  104.7 18.8 %fusion.55 = (bf16[2048,2,1408]{2,1,0:T(2,128)(2,1)}, bf16[2048,2,1408]{2,1,0:T(2,128)(2,1)}) fusion(bf16[2048,2,2816]{2,1,0:T(2,128)(2,1)} %param.32), kind=kLoop, calls=%fused_computation.115 | loop fusion | bytes 46137344 | tf_op jit(solution)/shard_map/slice | solution.py:267
  123.5 54.2 %all-to-all-done.1 = bf16[32,24,2048]{2,1,0:T(8,128)(2,1)} async-done(((bf16[32,24,2048]{2,1,0:T(8,128)(2,1)}), bf16[32,24,2048]{2,1,0:T(8,128)(2,1)}, u32[]{:S(2)}, u32[]{:S(2)}) %all-to-all-start.1) | async-done | bytes 3145760 | tf_op jit(solution)/shard_map/all_to_all | solution.py:261
  177.7 3.5 all-to-all-start
  181.3 14.8 %fusion.9 = f32[2,32,24,1408]{3,2,0,1:T(8,128)S(1)} fusion(bf16[2048,2,1408]{2,1,0:T(2,128)(2,1)} %get-tuple-element.35, bf16[32,24,2048]{2,1,0:T(8,128)(2,1)} %all-to-all-done.1), kind=kOutput, calls=%fused_computation.14 | convolution fusion | flops 8858370048 | bytes 23330816 | tf_op jit(solution)/shard_map/gsd,dju->jgsu/dot_general | solution.py:268
  196.1 9.6 %fusion.15 = bf16[32,24,2048]{2,1,0:T(8,128)(2,1)} fusion(bf16[2816,2048]{1,0:T(8,128)(2,1)} %param.33, f32[2,32,24,1408]{3,2,0,1:T(8,128)S(1)} %fusion.9), kind=kOutput, calls=%fused_computation.23 | convolution fusion | flops 4437245952 | bytes 17563648 | tf_op jit(solution)/shard_map/gsu,ud->gsd/dot_general | solution.py:272
  205.6 48.7 %all-to-all-done = bf16[32,24,2048]{2,1,0:T(8,128)(2,1)} async-done(((bf16[32,24,2048]{2,1,0:T(8,128)(2,1)}), bf16[32,24,2048]{2,1,0:T(8,128)(2,1)}, u32[]{:S(2)}, u32[]{:S(2)}) %all-to-all-start) | async-done | bytes 3145760 | tf_op jit(solution)/shard_map/all_to_all | solution.py:261
  254.4 14.9 %all-to-all-start.2 = ((bf16[32,24,2048]{2,1,0:T(8,128)(2,1)}), bf16[32,24,2048]{2,1,0:T(8,128)(2,1)}, u32[]{:S(2)}, u32[]{:S(2)}) async-start(bf16[32,24,2048]{2,1,0:T(8,128)(2,1)} %fusion.15), calls=%async_computation.2 | async-start | bytes 6291456 | tf_op jit(solution)/shard_map/all_to_all | solution.py:277
  269.3 14.8 %fusion.8 = f32[2,32,24,1408]{3,2,0,1:T(8,128)S(1)} fusion(bf16[2048,2,1408]{2,1,0:T(2,128)(2,1)} %get-tuple-element.34, bf16[32,24,2048]{2,1,0:T(8,128)(2,1)} %all-to-all-done), kind=kOutput, calls=%fused_computation.13 | convolution fusion | flops 8858370048 | bytes 23330816 | tf_op jit(solution)/shard_map/gsd,dju->jgsu/dot_general | solution.py:268
  284.1 9.5 %fusion.12 = bf16[32,24,2048]{2,1,0:T(8,128)(2,1)} fusion(bf16[2816,2048]{1,0:T(8,128)(2,1)} %param.33, f32[2,32,24,1408]{3,2,0,1:T(8,128)S(1)} %fusion.8), kind=kOutput, calls=%fused_computation.22 | convolution fusion | flops 4437245952 | bytes 17563648 | tf_op jit(solution)/shard_map/gsu,ud->gsd/dot_general | solution.py:272
  295.1 18.5 %collective-permute-done.4 = bf16[128,2048]{1,0:T(8,128)(2,1)S(1)} collective-permute-done((bf16[128,2048]{1,0:T(8,128)(2,1)S(1)}, bf16[128,2048]{1,0:T(8,128)(2,1)S(1)}, u32[]{:S(2)}, u32[]{:S(2)}) %collective-permute-start.4) | collective-permute-done | bytes 524320 | tf_op jit(solution)/shard_map/ppermute | solution.py:161
  317.5 24.5 %all-to-all-done.2 = bf16[32,24,2048]{2,1,0:T(8,128)(2,1)} async-done(((bf16[32,24,2048]{2,1,0:T(8,128)(2,1)}), bf16[32,24,2048]{2,1,0:T(8,128)(2,1)}, u32[]{:S(2)}, u32[]{:S(2)}) %all-to-all-start.2) | async-done | bytes 3145760 | tf_op jit(solution)/shard_map/all_to_all | solution.py:277
  342.0 3.5 all-to-all-start.3
  352.9 3.2 convolution_bitcast_fusion
  371.1 4.5 %fusion.58 = f32[128,2048]{1,0:T(8,128)} fusion(f32[128,768]{0,1:T(8,128)S(1)} %bitcast.211, bf16[768,2048]{1,0:T(8,128)(2,1)} %bitcast.49), kind=kOutput, calls=%fused_computation.118 | convolution fusion | flops 2415919104 | bytes 4587520 | tf_op jit(solution)/shard_map/dot_general | solution.py:279
  375.6 43.0 %all-to-all-done.3 = bf16[32,24,2048]{2,1,0:T(8,128)(2,1)} async-done(((bf16[32,24,2048]{2,1,0:T(8,128)(2,1)}), bf16[32,24,2048]{2,1,0:T(8,128)(2,1)}, u32[]{:S(2)}, u32[]{:S(2)}) %all-to-all-start.3) | async-done | bytes 3145760 | tf_op jit(solution)/shard_map/all_to_all | solution.py:277
  418.6 4.0 fusion.20
  (106 shorter events, 71.7 us)
Async XLA Ops:
  0.0 356.1 %copy-start = (bf16[704,2048]{1,0:T(8,128)(2,1)S(1)}, bf16[704,2048]{1,0:T(8,128)(2,1)}, u32[]{:S(2)}) copy-start(bf16[704,2048]{1,0:T(8,128)(2,1)} %param.28) | copy-start | bytes 8650756
  0.0 18.1 %copy-start.4 = (bf16[1,128,2048]{2,1,0:T(8,128)(2,1)S(1)}, bf16[1,128,2048]{2,1,0:T(8,128)(2,1)}, u32[]{:S(2)}) copy-start(bf16[1,128,2048]{2,1,0:T(8,128)(2,1)} %param.19) | copy-start | bytes 1572868
  0.0 18.1 %copy-start.11 = (f32[2048]{0:T(1024)S(1)}, f32[2048]{0:T(1024)}, u32[]{:S(2)}) copy-start(f32[2048]{0:T(1024)} %param.21) | copy-start | bytes 24580
  0.0 16.3 %copy-start.14 = (s32[64]{0:T(128)S(1)}, s32[64]{0:T(128)}, u32[]{:S(2)}) copy-start(s32[64]{0:T(128)} %param.31) | copy-start | bytes 772
  0.0 18.1 %copy-start.13 = (f32[1,128,6]{1,0,2:T(1,128)S(1)}, f32[1,128,6]{1,0,2:T(1,128)}, u32[]{:S(2)}) copy-start(f32[1,128,6]{1,0,2:T(1,128)} %param.30) | copy-start | bytes 9220
  3.4 15.2 %collective-permute-start = (bf16[128,2048]{1,0:T(8,128)(2,1)}, bf16[128,2048]{1,0:T(8,128)(2,1)}, u32[]{:S(2)}, u32[]{:S(2)}) collective-permute-start(bf16[128,2048]{1,0:T(8,128)(2,1)} %fusion.33), channel_id=1, source_target_pairs={{0,16},{8,24},{16,0},{24,8},{1,17},{9,25},{17,1},{25,9},{2,18},{10... | collective-permute-start | bytes 1572872 | tf_op jit(solution)/shard_map/ppermute | solution.py:161
  25.9 4.3 %collective-permute-start.1 = (bf16[2,128,2048]{2,1,0:T(8,128)(2,1)}, bf16[2,128,2048]{2,1,0:T(8,128)(2,1)}, u32[]{:S(2)}, u32[]{:S(2)}) collective-permute-start(bf16[2,128,2048]{2,1,0:T(8,128)(2,1)} %broadcast_select_fusion.1), channel_id=1, source_target_pairs={{0,8},{8,0},{16,24},{24,16},{1,9},{9,1},{17,25},{25,17},{2,10},{10... | collective-permute-start | bytes 3145736 | tf_op jit(solution)/shard_map/ppermute | solution.py:166
  26.1 4.1 copy-start.1
  30.3 2.5 slice-start
  68.4 3.1 collective-permute-start.2
  75.3 17.9 %copy-start.12 = (f32[2048]{0:T(1024)S(1)}, f32[2048]{0:T(1024)}, u32[]{:S(2)}) copy-start(f32[2048]{0:T(1024)} %param.26) | copy-start | bytes 24580
  76.2 14.5 %collective-permute-start.3 = (bf16[128,2048]{1,0:T(8,128)(2,1)}, bf16[128,2048]{1,0:T(8,128)(2,1)}, u32[]{:S(2)}, u32[]{:S(2)}) collective-permute-start(bf16[128,2048]{1,0:T(8,128)(2,1)} %bitcast_convert_fusion.1), channel_id=1, source_target_pairs={{0,16},{8,24},{16,0},{24,8},{1,17},{9,25},{17,1},{25,9},{2,18},{10... | collective-permute-start | bytes 1572872 | tf_op jit(solution)/shard_map/ppermute | solution.py:185
  77.9 15.5 %copy-start.10 = (bf16[128,1536]{1,0:T(8,128)(2,1)S(1)}, bf16[128,1536]{1,0:T(8,128)(2,1)}, u32[]{:S(2)}) copy-start(bf16[128,1536]{1,0:T(8,128)(2,1)} %get-tuple-element.13) | copy-start | bytes 1179652
  98.4 79.3 %all-to-all-start.1 = ((bf16[32,24,2048]{2,1,0:T(8,128)(2,1)}), bf16[32,24,2048]{2,1,0:T(8,128)(2,1)}, u32[]{:S(2)}, u32[]{:S(2)}) async-start(bf16[32,24,2048]{2,1,0:T(8,128)(2,1)} %get-tuple-element.37), calls=%async_computation.1 | async-start | bytes 6291456 | tf_op jit(solution)/shard_map/all_to_all | solution.py:261
  177.7 76.6 %all-to-all-start = ((bf16[32,24,2048]{2,1,0:T(8,128)(2,1)}), bf16[32,24,2048]{2,1,0:T(8,128)(2,1)}, u32[]{:S(2)}, u32[]{:S(2)}) async-start(bf16[32,24,2048]{2,1,0:T(8,128)(2,1)} %get-tuple-element.36), calls=%async_computation | async-start | bytes 6291456 | tf_op jit(solution)/shard_map/all_to_all | solution.py:261
  254.4 87.6 %all-to-all-start.2 = ((bf16[32,24,2048]{2,1,0:T(8,128)(2,1)}), bf16[32,24,2048]{2,1,0:T(8,128)(2,1)}, u32[]{:S(2)}, u32[]{:S(2)}) async-start(bf16[32,24,2048]{2,1,0:T(8,128)(2,1)} %fusion.15), calls=%async_computation.2 | async-start | bytes 6291456 | tf_op jit(solution)/shard_map/all_to_all | solution.py:277
  293.6 20.0 %collective-permute-start.4 = (bf16[128,2048]{1,0:T(8,128)(2,1)S(1)}, bf16[128,2048]{1,0:T(8,128)(2,1)S(1)}, u32[]{:S(2)}, u32[]{:S(2)}) collective-permute-start(bf16[128,2048]{1,0:T(8,128)(2,1)S(1)} %bitcast.207), channel_id=1, source_target_pairs={{0,16},{8,24},{16,0},{24,8},{1,17},{9,25},{17,1},{25,9},{2,18},{10... | collective-permute-start | bytes 1572872 | tf_op jit(solution)/shard_map/ppermute | solution.py:161
  342.0 76.6 %all-to-all-start.3 = ((bf16[32,24,2048]{2,1,0:T(8,128)(2,1)}), bf16[32,24,2048]{2,1,0:T(8,128)(2,1)}, u32[]{:S(2)}, u32[]{:S(2)}) async-start(bf16[32,24,2048]{2,1,0:T(8,128)(2,1)} %fusion.12), calls=%async_computation.3 | async-start | bytes 6291456 | tf_op jit(solution)/shard_map/all_to_all | solution.py:277
  346.9 2.7 collective-permute-start.5
  349.7 2.5 slice-start.2
  360.5 4.4 %collective-permute-start.6 = (bf16[2,128,2048]{2,1,0:T(8,128)(2,1)}, bf16[2,128,2048]{2,1,0:T(8,128)(2,1)}, u32[]{:S(2)}, u32[]{:S(2)}) collective-permute-start(bf16[2,128,2048]{2,1,0:T(8,128)(2,1)} %select_bitcast_fusion), channel_id=1, source_target_pairs={{0,8},{8,0},{16,24},{24,16},{1,9},{9,1},{17,25},{25,17},{2,10},{10... | collective-permute-start | bytes 3145736 | tf_op jit(solution)/shard_map/ppermute | solution.py:180
  369.5 53.1 %collective-permute-start.7 = (bf16[128,2048]{1,0:T(8,128)(2,1)}, bf16[128,2048]{1,0:T(8,128)(2,1)}, u32[]{:S(2)}, u32[]{:S(2)}) collective-permute-start(bf16[128,2048]{1,0:T(8,128)(2,1)} %bitcast_convert_fusion), channel_id=1, source_target_pairs={{0,16},{8,24},{16,0},{24,8},{1,17},{9,25},{17,1},{25,9},{2,18},{10... | collective-permute-start | bytes 1572872 | tf_op jit(solution)/shard_map/ppermute | solution.py:185
  375.6 47.0 %copy-start.9 = (bf16[1,128,2048]{2,1,0:T(8,128)(2,1)S(1)}, bf16[1,128,2048]{2,1,0:T(8,128)(2,1)}, u32[]{:S(2)}) copy-start(bf16[1,128,2048]{2,1,0:T(8,128)(2,1)} %copy-done.8) | copy-start | bytes 1572868
  418.6 4.0 copy-start.7
  (7 other events, 9.6 us)
